TPU v7x, 1024 devices: a whole 4x8x16 slice. The times are simulated.
1024 devices in a mesh: tensor: 16 (over x, y_lo), context: 32 (over z, y_hi), dp: 2 (over core).
Axes of the slice: x: 4, y: 8 (y_hi: 2, y_lo: 4; y = y_hi * 4 + y_lo), z: 16, core: 2. Of those that a mesh axis runs over, the one named last changes fastest.
Arguments:
- tokens: bfloat16 [2, 32, 128, 8192], P('dp', 'context', 'tensor'), may hold values from -6 to 6
- w_in: bfloat16 [8192, 2, 4096], P(None, None, 'tensor'), may hold values from -0.0625 to 0.0625
- gate: bfloat16 [2, 32, 128, 4096], P('dp', 'context', None, 'tensor'), may hold values from -6 to 6
- cotangent: bfloat16 [2, 32, 128, 4096], P('dp', 'context', None, 'tensor'), may hold values from -6 to 6
- filters: bfloat16 [256, 128], P('tensor'), may hold values from -0.5 to 0.5
Outputs:
- d_tokens: bfloat16 [2, 32, 128, 8192], P('dp', 'context', 'tensor')
- d_gate: bfloat16 [2, 32, 128, 4096], P('dp', 'context', None, 'tensor')
- d_filter: float32 [256, 128], P('tensor')
All inputs are finite; a program needn't handle non-finite values.
Results may differ from a plain program's by a relative error of at most 0.018.
Values may be sent and summed in bfloat16 or wider, within the bound.
No kernel may reach another device: no remote copies, remote signals or barrier semaphores. Data moves between devices by JAX's collectives and lax.ppermute only.
A program may use at most 64 MiB of HBM per device.

v0:
```python
import math

import jax
import jax.numpy as jnp
from jax import lax
from jax.sharding import PartitionSpec as P


def from_behind(value, axis, steps):
    count = lax.axis_size(axis)
    first, last = (max(0, -steps), min(count, count - steps))
    return lax.ppermute(value, axis, [(source, source + steps) for source in range(first, last)])


def skew_band(filters, stretch_rows):
    groups, tap_count = filters.shape
    band_width = stretch_rows + tap_count
    reversed_taps = filters[:, ::-1]
    pattern = jnp.concatenate(
        [
            jnp.zeros((groups, 1), filters.dtype),
            reversed_taps,
            jnp.zeros((groups, stretch_rows), filters.dtype),
        ],
        axis=1,
    )
    tiled = jnp.tile(pattern, (1, stretch_rows))[:, : stretch_rows * band_width]
    return tiled.reshape(groups, stretch_rows, band_width)


def band_sums(products, tap_count):
    groups, stretch_rows, band_width = products.shape
    flat_view = jnp.pad(
        products.reshape(groups, stretch_rows * band_width), ((0, 0), (0, stretch_rows))
    )
    folded = flat_view.reshape(groups, stretch_rows, band_width + 1).sum(axis=1)
    return folded[:, tap_count:0:-1]


def body(tokens, w_in, gate, cotangent, filters):
    seq_count = tokens.shape[0]
    model_width = tokens.shape[3]
    channels = w_in.shape[2]
    groups, tap_count = filters.shape
    group_size = channels // groups
    stretch_rows = gate.shape[2]
    weight_flat = w_in.reshape(model_width, 2 * channels)
    projected = jnp.einsum(
        "abnd,dc->abnc",
        lax.all_gather(tokens, "tensor", axis=2, tiled=True),
        weight_flat,
        preferred_element_type=jnp.float32,
    ).astype(jnp.bfloat16)[:, 0]
    second_in = projected[..., :channels].astype(jnp.float32)
    value_in = projected[..., channels:].astype(jnp.float32)
    mixed = (second_in * value_in).astype(jnp.bfloat16)
    gate_rows = gate[:, 0].astype(jnp.float32)
    grad_out = cotangent[:, 0].astype(jnp.float32)
    grad_mix = (grad_out * gate_rows).astype(jnp.bfloat16)
    prev_rows = from_behind(mixed[:, stretch_rows - (tap_count - 1) :], "context", 1)
    extended = jnp.concatenate(
        [jnp.zeros((seq_count, 1, channels), jnp.bfloat16), prev_rows, mixed], axis=1
    )
    extended = extended.reshape(seq_count, stretch_rows + tap_count, groups, group_size)
    toeplitz = skew_band(filters, stretch_rows)
    conv_out = jnp.einsum("gts,bsgc->btgc", toeplitz, extended, preferred_element_type=jnp.float32)
    conv_out = conv_out.reshape(seq_count, stretch_rows, channels)
    d_gate = (grad_out * conv_out).astype(jnp.bfloat16)[:, None]
    grad_blocks = grad_mix.reshape(seq_count, stretch_rows, groups, group_size)
    spread = jnp.einsum("gts,btgc->bsgc", toeplitz, grad_blocks, preferred_element_type=jnp.float32)
    own_part = spread[:, tap_count:]
    next_rows_in = from_behind(grad_mix[:, : tap_count - 1], "context", -1)
    next_blocks = next_rows_in.reshape(seq_count, tap_count - 1, groups, group_size)
    from_next = jnp.einsum(
        "gts,btgc->bsgc",
        toeplitz[:, : tap_count - 1, 1:tap_count],
        next_blocks,
        preferred_element_type=jnp.float32,
    )
    split_at = stretch_rows - tap_count + 1
    grad_conv = jnp.concatenate(
        [own_part[:, :split_at], own_part[:, split_at:] + from_next], axis=1
    )
    grad_conv = grad_conv.reshape(seq_count, stretch_rows, channels)
    grad_in = jnp.concatenate([grad_conv * value_in, grad_conv * second_in], axis=-1).astype(
        jnp.bfloat16
    )
    partials = jnp.einsum("bnc,dc->bnd", grad_in, weight_flat, preferred_element_type=jnp.float32)
    d_tokens = lax.psum_scatter(
        partials.astype(jnp.bfloat16), "tensor", scatter_dimension=1, tiled=True
    ).astype(jnp.float32)
    d_tokens = d_tokens.astype(jnp.bfloat16)[:, None]
    products = jnp.einsum(
        "btgc,bsgc->gts", grad_blocks, extended, preferred_element_type=jnp.float32
    )
    local_grad = band_sums(products, tap_count)
    summed = lax.psum(local_grad, ("context", "dp"))
    term_total = (
        seq_count * lax.axis_size("dp") * stretch_rows * lax.axis_size("context") * group_size
    )
    d_filter = summed * (1.0 / math.sqrt(term_total))
    return (d_tokens, d_gate, d_filter)


def solution(mesh):
    return jax.shard_map(
        body,
        mesh=mesh,
        in_specs=(
            P("dp", "context", "tensor", None),
            P(None, None, "tensor"),
            P("dp", "context", None, "tensor"),
            P("dp", "context", None, "tensor"),
            P("tensor", None),
        ),
        out_specs=(
            P("dp", "context", "tensor", None),
            P("dp", "context", None, "tensor"),
            P("tensor", None),
        ),
        check_vma=False,
    )
```

profile of v0, /device:TPU:1, one launch (start us, length us, event | category | flops | bytes accessed | tf_op | source)
XLA Modules:
  0.0 323.0 jit_solution(12147588290070846426)
XLA Ops:
  7.2 0.7 all-gather.2.cloned.1.call-update
  7.9 0.9 copy.16
  8.9 1.0 copy.17
  9.9 1.3 collective-permute-start
  11.2 0.8 rev.6
  12.3 1.8 tile.10
  14.2 0.2 copy.22
  14.4 0.3 convolution_bitcast_fusion
  14.7 8.0 %copy.23 = bf16[1024,8,2,256]{3,1,2,0:T(8,128)(2,1)} copy(bf16[1024,8,2,256]{3,2,1,0:T(2,128)(2,1)} %bitcast.61) | data formatting | bytes 16777216
  22.7 0.3 fusion.6
  23.3 81.8 %all-gather.2.cloned.1.call-done = bf16[1,1,128,8192]{3,2,1,0:T(8,128)(2,1)} async-done(((bf16[1,1,8,8192]{3,2,1,0:T(8,128)(2,1)}), bf16[1,1,128,8192]{3,2,1,0:T(8,128)(2,1)}) %all-gather.2.cloned.1.call-update) | async-done | bytes 2097168 | tf_op jit(solution)/shard_map/all_gather | solution.py:50
  105.1 5.4 %fusion.7 = bf16[1,128,512]{2,1,0:T(8,128)(2,1)S(1)} fusion(bf16[8192,512]{1,0:T(8,128)(2,1)} %bitcast.54, bf16[1,1,128,8192]{3,2,1,0:T(8,128)(2,1)} %all-gather.2.cloned.1.call-done), kind=kOutput, calls=%fused_computation.8 | convolution fusion | flops 1073807360 | bytes 10616832 | tf_op jit(solution)/shard_map/abnd,dc->abnc/dot_general | solution.py:48
  110.6 1.0 slice-done.1
  111.6 4.1 %fusion = bf16[1,128,8192]{2,1,0:T(8,128)(2,1)} fusion(bf16[8192,512]{1,0:T(8,128)(2,1)S(1)} %bitcast.57, bf16[128,256]{1,0:T(8,128)(2,1)S(1)} %get-tuple-element.7, bf16[128,256]{1,0:T(8,128)(2,1)S(1)} %get-tuple-element.6), kind=kOutput, calls=%fused_computation.1 | convolution fusion | flops 1075052544 | bytes 10616832 | tf_op jit(solution)/shard_map/bnc,dc->bnd/dot_general | solution.py:88
  115.8 4.7 %collective-permute-start.1 = (bf16[1,127,256]{2,1,0:T(8,128)(2,1)S(1)}, bf16[1,127,256]{2,1,0:T(8,128)(2,1)S(1)}, u32[]{:S(2)}, u32[]{:S(2)}) collective-permute-start(bf16[1,127,256]{2,1,0:T(8,128)(2,1)S(1)} %slice.46), channel_id=1, source_target_pairs={{0,2},{2,4},{4,6},{6,8},{8,10},{10,12},{12,14},{14,16},{16,18},{18... | collective-permute-start | bytes 195080 | tf_op jit(solution)/shard_map/ppermute | solution.py:12
  120.5 1.3 collective-permute-done.1
  122.0 0.4 fusion.22
  122.4 0.7 copy.21
  123.2 0.5 fusion.23
  123.7 1.2 copy.24
  124.9 1.5 pad.4
  126.4 3.7 %reshape.128 = f32[16,128,257]{2,1,0:T(8,128)S(1)} reshape(f32[16,32896]{1,0:T(8,128)} %pad.4) | data formatting | bytes 4210688 | tf_op jit(solution)/shard_map/reshape | solution.py:36
  130.5 185.1 %psum.7 = f32[16,128]{1,0:T(8,128)S(1)} all-reduce(f32[16,128]{1,0:T(8,128)S(1)} %rev.7), channel_id=1, replica_groups=mesh['tensor'=16,'context'=32,'dp'=2] {'context','dp'}, use_global_device_ids=true, to_apply=%region_2.3 | all-reduce | flops 2048 | bytes 16384 | tf_op jit(solution)/shard_map/psum | solution.py:97
  315.6 0.6 broadcast_multiply_fusion
  (28 shorter events, 1.4 us)
Async XLA Ops:
  7.2 98.0 %all-gather.2.cloned.1.call-start = ((), (), s32[]{:S(2)}) async-start(), calls=%async_computation.1 | async-start | bytes 2228224 | tf_op jit(solution)/shard_map/all_gather | solution.py:50
  7.9 308.3 %reduce-scatter.2.cloned.1.call-start = ((), (), s32[]{:S(2)}) async-start(), calls=%async_computation.2 | async-start | bytes 2228224 | tf_op jit(solution)/shard_map/reduce_scatter | solution.py:89
  9.9 12.8 %collective-permute-start = (bf16[1,127,256]{1,2,0:T(8,128)(2,1)S(1)}, bf16[1,127,256]{1,2,0:T(8,128)(2,1)S(1)}, u32[]{:S(2)}, u32[]{:S(2)}) collective-permute-start(bf16[1,127,256]{1,2,0:T(8,128)(2,1)S(1)} %bitcast.67), channel_id=1, source_target_pairs={{2,0},{4,2},{6,4},{8,6},{10,8},{12,10},{14,12},{16,14},{18,16},{20... | collective-permute-start | bytes 195080 | tf_op jit(solution)/shard_map/ppermute | solution.py:12
  105.1 5.5 %slice-start = ((s8[8388608]{0:T(1024)(128)(4,1)}), s8[4194304]{0:T(1024)(128)(4,1)S(1)}, s32[]{:S(2)}) async-start(s8[8388608]{0:T(1024)(128)(4,1)} %bitcast.55), calls=%async_computation.3 | async-start | bytes 8388608
  105.1 6.5 %slice-start.1 = ((s8[8388608]{0:T(1024)(128)(4,1)}), s8[4194304]{0:T(1024)(128)(4,1)S(1)}, s32[]{:S(2)}) async-start(s8[8388608]{0:T(1024)(128)(4,1)} %bitcast.55), calls=%async_computation.4 | async-start | bytes 8388608
  115.8 6.0 %collective-permute-start.1 = (bf16[1,127,256]{2,1,0:T(8,128)(2,1)S(1)}, bf16[1,127,256]{2,1,0:T(8,128)(2,1)S(1)}, u32[]{:S(2)}, u32[]{:S(2)}) collective-permute-start(bf16[1,127,256]{2,1,0:T(8,128)(2,1)S(1)} %slice.46), channel_id=1, source_target_pairs={{0,2},{2,4},{4,6},{6,8},{8,10},{10,12},{12,14},{14,16},{16,18},{18... | collective-permute-start | bytes 195080 | tf_op jit(solution)/shard_map/ppermute | solution.py:12
Sparse Core Ops, SparseCore 0:
  10.6 94.4 all-gather.1
  115.9 98.5 reduce-scatter.1
where the time goes:
time: 323 us
  blocking collectives  185 us (57%)
  waiting for transfers between devices  83.8 us (26%)
  local copies, waits for them, and re-layouts  21.6 us (7%)
  between operations  14.2 us (4%)
  matrix products  11 us (3%)
  starting transfers between devices  6.08 us (2%)
    psum x1, blocking collectives, body(): summed = lax.psum(local_grad, ('context', 'dp'))  185 us
    all_gather x1, waiting for transfers between devices, body(): lax.all_gather(tokens, 'tensor', axis=2, tiled=True)  81.8 us
    unnamed x10, local copies, waits for them, and re-layouts  13.1 us
  transfers between devices with their start and end apart: 4, of which 2 were waited for; matrix products, arithmetic and copies ran while one was open for 7% of the time, Pallas kernels for 0%

commit v1 on v0

--- a/solution.py
+++ b/solution.py
@@ -10,6 +10,17 @@
     count = lax.axis_size(axis)
     first, last = (max(0, -steps), min(count, count - steps))
     return lax.ppermute(value, axis, [(source, source + steps) for source in range(first, last)])
+
+
+def butterfly_sum(value, axis):
+    count = lax.axis_size(axis)
+    if count & (count - 1):
+        return lax.psum(value, axis)
+    step = 1
+    while step < count:
+        value = value + lax.ppermute(value, axis, [(i, i ^ step) for i in range(count)])
+        step *= 2
+    return value
 
 
 def skew_band(filters, stretch_rows):
@@ -94,7 +105,7 @@
         "btgc,bsgc->gts", grad_blocks, extended, preferred_element_type=jnp.float32
     )
     local_grad = band_sums(products, tap_count)
-    summed = lax.psum(local_grad, ("context", "dp"))
+    summed = butterfly_sum(butterfly_sum(local_grad, "dp"), "context")
     term_total = (
         seq_count * lax.axis_size("dp") * stretch_rows * lax.axis_size("context") * group_size
     )

time: 323 us -> 230 us (0.71)
  the two profiles are of different devices: /device:TPU:1 before, /device:TPU:64 now
where the time goes in v1:
time: 230 us
  waiting for transfers between devices  133 us (58%)
  starting transfers between devices  48.3 us (21%)
  local copies, waits for them, and re-layouts  20.2 us (9%)
  between operations  14.3 us (6%)
  matrix products  11 us (5%)
  other arithmetic  3.19 us (1%)
    all_gather x1, waiting for transfers between devices, body(): lax.all_gather(tokens, 'tensor', axis=2, tiled=True)  83.6 us
    ppermute x6, starting transfers between devices, butterfly_sum(): lax.ppermute(value, axis, [(i, i ^ step) for i in range(count)])  34.4 us
    reduce_scatter x1, waiting for transfers between devices, body(): lax.psum_scatter(partials.astype(jnp.bfloat16), 'tensor', scatter_dimensi...  31.6 us
    ppermute x2, starting transfers between devices, from_behind(): lax.ppermute(value, axis, [(source, source + steps) for source in range(f...  13.8 us
    unnamed x10, local copies, waits for them, and re-layouts  13.1 us
    ppermute x6, waiting for transfers between devices, butterfly_sum(): lax.ppermute(value, axis, [(i, i ^ step) for i in range(count)])  12.6 us
    dot_general x1, matrix products, body(): jnp.einsum('abnd,dc->abnc', lax.all_gather(tokens, 'tensor', axis=2, tile...  5.41 us
  transfers between devices with their start and end apart: 10, of which 9 were waited for; matrix products, arithmetic and copies ran while one was open for 10% of the time, Pallas kernels for 0%

profile of v1, /device:TPU:64, one launch (start us, length us, event | category | flops | bytes accessed | tf_op | source)
XLA Modules:
  0.0 230.0 jit_solution(17650942955149721786)
XLA Ops:
  9.9 6.8 %collective-permute-start = (bf16[1,127,256]{1,2,0:T(8,128)(2,1)S(1)}, bf16[1,127,256]{1,2,0:T(8,128)(2,1)S(1)}, u32[]{:S(2)}, u32[]{:S(2)}) collective-permute-start(bf16[1,127,256]{1,2,0:T(8,128)(2,1)S(1)} %bitcast.67), channel_id=1, source_target_pairs={{2,0},{4,2},{6,4},{8,6},{10,8},{12,10},{14,12},{16,14},{18,16},{20... | collective-permute-start | bytes 195080 | tf_op jit(solution)/shard_map/ppermute | solution.py:12
  17.8 1.8 tile.10
  20.2 8.0 %copy.23 = bf16[1024,8,2,256]{3,1,2,0:T(8,128)(2,1)} copy(bf16[1024,8,2,256]{3,2,1,0:T(2,128)(2,1)} %bitcast.61) | data formatting | bytes 16777216
  28.8 83.6 %all-gather.2.cloned.1.call-done = bf16[1,1,128,8192]{3,2,1,0:T(8,128)(2,1)} async-done(((bf16[1,1,8,8192]{3,2,1,0:T(8,128)(2,1)}), bf16[1,1,128,8192]{3,2,1,0:T(8,128)(2,1)}) %all-gather.2.cloned.1.call-update) | async-done | bytes 2097168 | tf_op jit(solution)/shard_map/all_gather | solution.py:61
  112.4 5.4 %fusion.7 = bf16[1,128,512]{2,1,0:T(8,128)(2,1)S(1)} fusion(bf16[8192,512]{1,0:T(8,128)(2,1)} %bitcast.54, bf16[1,1,128,8192]{3,2,1,0:T(8,128)(2,1)} %all-gather.2.cloned.1.call-done), kind=kOutput, calls=%fused_computation.8 | convolution fusion | flops 1073807360 | bytes 10616832 | tf_op jit(solution)/shard_map/abnd,dc->abnc/dot_general | solution.py:59
  117.9 1.0 slice-done.1
  118.9 4.2 %fusion = bf16[1,128,8192]{2,1,0:T(8,128)(2,1)} fusion(bf16[8192,512]{1,0:T(8,128)(2,1)S(1)} %bitcast.57, bf16[128,256]{1,0:T(8,128)(2,1)S(1)} %get-tuple-element.7, bf16[128,256]{1,0:T(8,128)(2,1)S(1)} %get-tuple-element.6), kind=kOutput, calls=%fused_computation.1 | convolution fusion | flops 1075052544 | bytes 10616832 | tf_op jit(solution)/shard_map/bnc,dc->bnd/dot_general | solution.py:99
  123.1 7.0 %collective-permute-start.1 = (bf16[1,127,256]{2,1,0:T(8,128)(2,1)S(1)}, bf16[1,127,256]{2,1,0:T(8,128)(2,1)S(1)}, u32[]{:S(2)}, u32[]{:S(2)}) collective-permute-start(bf16[1,127,256]{2,1,0:T(8,128)(2,1)S(1)} %slice.46), channel_id=1, source_target_pairs={{0,2},{2,4},{4,6},{6,8},{8,10},{10,12},{12,14},{14,16},{16,18},{18... | collective-permute-start | bytes 195080 | tf_op jit(solution)/shard_map/ppermute | solution.py:12
  130.2 4.5 %collective-permute-done.1 = bf16[1,127,256]{2,1,0:T(8,128)(2,1)S(1)} collective-permute-done((bf16[1,127,256]{2,1,0:T(8,128)(2,1)S(1)}, bf16[1,127,256]{2,1,0:T(8,128)(2,1)S(1)}, u32[]{:S(2)}, u32[]{:S(2)}) %collective-permute-start.1) | collective-permute-done | bytes 65056 | tf_op jit(solution)/shard_map/ppermute | solution.py:12
  135.4 1.2 copy.24
  136.7 3.6 %reshape.128 = f32[16,128,257]{2,1,0:T(8,128)} reshape(f32[16,32896]{1,0:T(8,128)S(1)} %pad.4) | data formatting | bytes 4210688 | tf_op jit(solution)/shard_map/reshape | solution.py:47
  140.4 2.2 reduce_sum.9
  142.7 1.9 collective-permute-start.2
  144.6 1.1 collective-permute-done.2
  145.8 5.5 %collective-permute-start.3 = (f32[16,128]{1,0:T(8,128)S(1)}, f32[16,128]{1,0:T(8,128)S(1)}, u32[]{:S(2)}, u32[]{:S(2)}) collective-permute-start(f32[16,128]{1,0:T(8,128)S(1)} %add.26), channel_id=1, source_target_pairs={{0,2},{2,0},{4,6},{6,4},{8,10},{10,8},{12,14},{14,12},{16,18},{18,... | collective-permute-start | bytes 24584 | tf_op jit(solution)/shard_map/ppermute | solution.py:21
  151.2 4.0 %collective-permute-done.3 = f32[16,128]{1,0:T(8,128)S(1)} collective-permute-done((f32[16,128]{1,0:T(8,128)S(1)}, f32[16,128]{1,0:T(8,128)S(1)}, u32[]{:S(2)}, u32[]{:S(2)}) %collective-permute-start.3) | collective-permute-done | bytes 8224 | tf_op jit(solution)/shard_map/ppermute | solution.py:21
  155.2 1.9 collective-permute-start.4
  157.1 3.6 %collective-permute-done.4 = f32[16,128]{1,0:T(8,128)S(1)} collective-permute-done((f32[16,128]{1,0:T(8,128)S(1)}, f32[16,128]{1,0:T(8,128)S(1)}, u32[]{:S(2)}, u32[]{:S(2)}) %collective-permute-start.4) | collective-permute-done | bytes 8224 | tf_op jit(solution)/shard_map/ppermute | solution.py:21
  160.7 4.8 %collective-permute-start.5 = (f32[16,128]{1,0:T(8,128)S(1)}, f32[16,128]{1,0:T(8,128)S(1)}, u32[]{:S(2)}, u32[]{:S(2)}) collective-permute-start(f32[16,128]{1,0:T(8,128)S(1)} %add.28), channel_id=1, source_target_pairs={{0,8},{2,10},{4,12},{6,14},{8,0},{10,2},{12,4},{14,6},{16,24},{18,... | collective-permute-start | bytes 24584 | tf_op jit(solution)/shard_map/ppermute | solution.py:21
  165.5 1.7 collective-permute-done.5
  167.2 7.7 %collective-permute-start.6 = (f32[16,128]{1,0:T(8,128)S(1)}, f32[16,128]{1,0:T(8,128)S(1)}, u32[]{:S(2)}, u32[]{:S(2)}) collective-permute-start(f32[16,128]{1,0:T(8,128)S(1)} %add.29), channel_id=1, source_target_pairs={{0,16},{2,18},{4,20},{6,22},{8,24},{10,26},{12,28},{14,30},{16,0},... | collective-permute-start | bytes 24584 | tf_op jit(solution)/shard_map/ppermute | solution.py:21
  175.3 1.3 collective-permute-done.6
  176.6 12.6 %collective-permute-start.7 = (f32[16,128]{1,0:T(8,128)S(1)}, f32[16,128]{1,0:T(8,128)S(1)}, u32[]{:S(2)}, u32[]{:S(2)}) collective-permute-start(f32[16,128]{1,0:T(8,128)S(1)} %add.30), channel_id=1, source_target_pairs={{0,32},{2,34},{4,36},{6,38},{8,40},{10,42},{12,44},{14,46},{16,48}... | collective-permute-start | bytes 24584 | tf_op jit(solution)/shard_map/ppermute | solution.py:21
  191.5 31.6 %reduce-scatter.2.cloned.1.call-done = bf16[1,8,8192]{2,1,0:T(8,128)(2,1)} async-done(((bf16[1,128,8192]{2,1,0:T(8,128)(2,1)}), bf16[1,8,8192]{2,1,0:T(8,128)(2,1)}) %reduce-scatter.2.cloned.1.call-update) | async-done | bytes 131088 | tf_op jit(solution)/shard_map/reduce_scatter | solution.py:100
  (44 shorter events, 8.5 us)
Async XLA Ops:
  7.2 105.3 %all-gather.2.cloned.1.call-start = ((), (), s32[]{:S(2)}) async-start(), calls=%async_computation.1 | async-start | bytes 2228224 | tf_op jit(solution)/shard_map/all_gather | solution.py:61
  7.9 215.2 %reduce-scatter.2.cloned.1.call-start = ((), (), s32[]{:S(2)}) async-start(), calls=%async_computation.2 | async-start | bytes 2228224 | tf_op jit(solution)/shard_map/reduce_scatter | solution.py:100
  9.9 18.4 %collective-permute-start = (bf16[1,127,256]{1,2,0:T(8,128)(2,1)S(1)}, bf16[1,127,256]{1,2,0:T(8,128)(2,1)S(1)}, u32[]{:S(2)}, u32[]{:S(2)}) collective-permute-start(bf16[1,127,256]{1,2,0:T(8,128)(2,1)S(1)} %bitcast.67), channel_id=1, source_target_pairs={{2,0},{4,2},{6,4},{8,6},{10,8},{12,10},{14,12},{16,14},{18,16},{20... | collective-permute-start | bytes 195080 | tf_op jit(solution)/shard_map/ppermute | solution.py:12
  112.4 5.5 %slice-start = ((s8[8388608]{0:T(1024)(128)(4,1)}), s8[4194304]{0:T(1024)(128)(4,1)S(1)}, s32[]{:S(2)}) async-start(s8[8388608]{0:T(1024)(128)(4,1)} %bitcast.55), calls=%async_computation.3 | async-start | bytes 8388608
  112.4 6.5 %slice-start.1 = ((s8[8388608]{0:T(1024)(128)(4,1)}), s8[4194304]{0:T(1024)(128)(4,1)S(1)}, s32[]{:S(2)}) async-start(s8[8388608]{0:T(1024)(128)(4,1)} %bitcast.55), calls=%async_computation.4 | async-start | bytes 8388608
  123.1 11.5 %collective-permute-start.1 = (bf16[1,127,256]{2,1,0:T(8,128)(2,1)S(1)}, bf16[1,127,256]{2,1,0:T(8,128)(2,1)S(1)}, u32[]{:S(2)}, u32[]{:S(2)}) collective-permute-start(bf16[1,127,256]{2,1,0:T(8,128)(2,1)S(1)} %slice.46), channel_id=1, source_target_pairs={{0,2},{2,4},{4,6},{6,8},{8,10},{10,12},{12,14},{14,16},{16,18},{18... | collective-permute-start | bytes 195080 | tf_op jit(solution)/shard_map/ppermute | solution.py:12
  142.7 3.1 %collective-permute-start.2 = (f32[16,128]{1,0:T(8,128)S(1)}, f32[16,128]{1,0:T(8,128)S(1)}, u32[]{:S(2)}, u32[]{:S(2)}) collective-permute-start(f32[16,128]{1,0:T(8,128)S(1)} %rev.7), channel_id=1, source_target_pairs={{0,1},{1,0},{2,3},{3,2},{4,5},{5,4},{6,7},{7,6},{8,9},{9,8},{10,11... | collective-permute-start | bytes 24584 | tf_op jit(solution)/shard_map/ppermute | solution.py:21
  145.8 9.4 %collective-permute-start.3 = (f32[16,128]{1,0:T(8,128)S(1)}, f32[16,128]{1,0:T(8,128)S(1)}, u32[]{:S(2)}, u32[]{:S(2)}) collective-permute-start(f32[16,128]{1,0:T(8,128)S(1)} %add.26), channel_id=1, source_target_pairs={{0,2},{2,0},{4,6},{6,4},{8,10},{10,8},{12,14},{14,12},{16,18},{18,... | collective-permute-start | bytes 24584 | tf_op jit(solution)/shard_map/ppermute | solution.py:21
  155.2 5.5 %collective-permute-start.4 = (f32[16,128]{1,0:T(8,128)S(1)}, f32[16,128]{1,0:T(8,128)S(1)}, u32[]{:S(2)}, u32[]{:S(2)}) collective-permute-start(f32[16,128]{1,0:T(8,128)S(1)} %add.27), channel_id=1, source_target_pairs={{0,4},{2,6},{4,0},{6,2},{8,12},{10,14},{12,8},{14,10},{16,20},{18,... | collective-permute-start | bytes 24584 | tf_op jit(solution)/shard_map/ppermute | solution.py:21
  160.7 6.4 %collective-permute-start.5 = (f32[16,128]{1,0:T(8,128)S(1)}, f32[16,128]{1,0:T(8,128)S(1)}, u32[]{:S(2)}, u32[]{:S(2)}) collective-permute-start(f32[16,128]{1,0:T(8,128)S(1)} %add.28), channel_id=1, source_target_pairs={{0,8},{2,10},{4,12},{6,14},{8,0},{10,2},{12,4},{14,6},{16,24},{18,... | collective-permute-start | bytes 24584 | tf_op jit(solution)/shard_map/ppermute | solution.py:21
  167.2 9.4 %collective-permute-start.6 = (f32[16,128]{1,0:T(8,128)S(1)}, f32[16,128]{1,0:T(8,128)S(1)}, u32[]{:S(2)}, u32[]{:S(2)}) collective-permute-start(f32[16,128]{1,0:T(8,128)S(1)} %add.29), channel_id=1, source_target_pairs={{0,16},{2,18},{4,20},{6,22},{8,24},{10,26},{12,28},{14,30},{16,0},... | collective-permute-start | bytes 24584 | tf_op jit(solution)/shard_map/ppermute | solution.py:21
  176.6 14.3 %collective-permute-start.7 = (f32[16,128]{1,0:T(8,128)S(1)}, f32[16,128]{1,0:T(8,128)S(1)}, u32[]{:S(2)}, u32[]{:S(2)}) collective-permute-start(f32[16,128]{1,0:T(8,128)S(1)} %add.30), channel_id=1, source_target_pairs={{0,32},{2,34},{4,36},{6,38},{8,40},{10,42},{12,44},{14,46},{16,48}... | collective-permute-start | bytes 24584 | tf_op jit(solution)/shard_map/ppermute | solution.py:21
Sparse Core Ops, SparseCore 0:
  10.6 101.7 all-gather.1
  123.2 99.8 reduce-scatter.1

commit v2 on v1

--- a/solution.py
+++ b/solution.py
@@ -21,6 +21,46 @@
         value = value + lax.ppermute(value, axis, [(i, i ^ step) for i in range(count)])
         step *= 2
     return value
+
+
+def grid_shift(axis, steps, inner, outer_step):
+    count = lax.axis_size(axis)
+    if outer_step:
+        return [(i, ((i // inner + steps) % (count // inner)) * inner + i % inner) for i in range(count)]
+    return [(i, (i // inner) * inner + (i % inner + steps) % inner) for i in range(count)]
+
+
+def grid_gather(rows, axis, inner):
+    count = lax.axis_size(axis)
+    outer = count // inner
+    index = lax.axis_index(axis)
+    pieces = [rows] + [
+        lax.ppermute(rows, axis, grid_shift(axis, s, inner, False)) for s in range(1, inner)
+    ]
+    order = (index % inner - jnp.arange(inner)) % inner
+    stage = jnp.take(jnp.stack(pieces), order, axis=0)
+    pieces = [stage] + [
+        lax.ppermute(stage, axis, grid_shift(axis, s, inner, True)) for s in range(1, outer)
+    ]
+    order = (index // inner - jnp.arange(outer)) % outer
+    return jnp.take(jnp.stack(pieces), order, axis=0).reshape((count * rows.shape[0],) + rows.shape[1:])
+
+
+def grid_reduce_scatter(partial_rows, axis, inner):
+    count = lax.axis_size(axis)
+    outer = count // inner
+    index = lax.axis_index(axis)
+    chunks = partial_rows.reshape((outer, -1) + partial_rows.shape[1:])
+    acc = jnp.take(chunks, index // inner, axis=0).astype(jnp.float32)
+    for s in range(1, outer):
+        sent = jnp.take(chunks, (index // inner + s) % outer, axis=0)
+        acc = acc + lax.ppermute(sent, axis, grid_shift(axis, s, inner, True)).astype(jnp.float32)
+    chunks = acc.reshape((inner, -1) + acc.shape[1:])
+    total = jnp.take(chunks, index % inner, axis=0)
+    for s in range(1, inner):
+        sent = jnp.take(chunks, (index % inner + s) % inner, axis=0)
+        total = total + lax.ppermute(sent, axis, grid_shift(axis, s, inner, False))
+    return total
 
 
 def skew_band(filters, stretch_rows):
@@ -56,12 +96,11 @@
     group_size = channels // groups
     stretch_rows = gate.shape[2]
     weight_flat = w_in.reshape(model_width, 2 * channels)
+    inner = 4 if lax.axis_size("tensor") % 4 == 0 else 1
+    block_rows = grid_gather(tokens.reshape(tokens.shape[2], model_width), "tensor", inner)
     projected = jnp.einsum(
-        "abnd,dc->abnc",
-        lax.all_gather(tokens, "tensor", axis=2, tiled=True),
-        weight_flat,
-        preferred_element_type=jnp.float32,
-    ).astype(jnp.bfloat16)[:, 0]
+        "nd,dc->nc", block_rows, weight_flat, preferred_element_type=jnp.float32
+    ).astype(jnp.bfloat16)[None]
     second_in = projected[..., :channels].astype(jnp.float32)
     value_in = projected[..., channels:].astype(jnp.float32)
     mixed = (second_in * value_in).astype(jnp.bfloat16)
@@ -97,10 +136,8 @@
         jnp.bfloat16
     )
     partials = jnp.einsum("bnc,dc->bnd", grad_in, weight_flat, preferred_element_type=jnp.float32)
-    d_tokens = lax.psum_scatter(
-        partials.astype(jnp.bfloat16), "tensor", scatter_dimension=1, tiled=True
-    ).astype(jnp.float32)
-    d_tokens = d_tokens.astype(jnp.bfloat16)[:, None]
+    d_tokens = grid_reduce_scatter(partials[0].astype(jnp.bfloat16), "tensor", inner)
+    d_tokens = d_tokens.astype(jnp.bfloat16)[None, None]
     products = jnp.einsum(
         "btgc,bsgc->gts", grad_blocks, extended, preferred_element_type=jnp.float32
     )

time: 230 us -> 197 us (0.86)
  the two profiles are of different devices: /device:TPU:64 before, /device:TPU:40 now
where the time goes in v2:
time: 197 us; the launch traced here: 196 us
  starting transfers between devices  99.4 us (50%)
  local copies, waits for them, and re-layouts  38.5 us (20%)
  waiting for transfers between devices  38 us (19%)
  other arithmetic  9.59 us (5%)
  matrix products  9.15 us (5%)
    ppermute x6, starting transfers between devices, butterfly_sum(): lax.ppermute(value, axis, [(i, i ^ step) for i in range(count)])  41.5 us
    ppermute x2, starting transfers between devices, from_behind(): lax.ppermute(value, axis, [(source, source + steps) for source in range(f...  18.4 us
    reshape x1, local copies, waits for them, and re-layouts, body(): weight_flat = w_in.reshape(model_width, 2 * channels)  14.1 us
    ppermute x3, waiting for transfers between devices, grid_reduce_scatter(): total = total + lax.ppermute(sent, axis, grid_shift(axis, s, inner, False))  13.7 us
    unnamed x16, local copies, waits for them, and re-layouts  13.5 us
    ppermute x3, waiting for transfers between devices, grid_gather(): lax.ppermute(stage, axis, grid_shift(axis, s, inner, True))  12.8 us
    ppermute x3, starting transfers between devices, grid_reduce_scatter(): lax.ppermute(sent, axis, grid_shift(axis, s, inner, True))  11.6 us
    ppermute x6, waiting for transfers between devices, butterfly_sum(): lax.ppermute(value, axis, [(i, i ^ step) for i in range(count)])  11.4 us
  transfers between devices with their start and end apart: 20, of which 9 were waited for; matrix products, arithmetic and copies ran while one was open for 22% of the time, Pallas kernels for 0%

profile of v2, /device:TPU:40, one launch (start us, length us, event | category | flops | bytes accessed | tf_op | source)
XLA Modules:
  0.0 196.1 jit_solution(754228444210498470)
XLA Ops:
  3.2 4.9 %collective-permute-start.2 = (bf16[8,8192]{1,0:T(8,128)(2,1)}, bf16[8,8192]{1,0:T(8,128)(2,1)S(1)}, u32[]{:S(2)}, u32[]{:S(2)}) collective-permute-start(bf16[8,8192]{1,0:T(8,128)(2,1)} %bitcast.110), channel_id=1, source_target_pairs={{0,128},{64,192},{128,0},{192,64},{256,384},{320,448},{384,256},{4... | collective-permute-start | bytes 393224 | tf_op jit(solution)/shard_map/ppermute | solution.py:38
  12.1 14.6 %collective-permute-start = (bf16[1,127,256]{1,2,0:T(8,128)(2,1)S(1)}, bf16[1,127,256]{1,2,0:T(8,128)(2,1)S(1)}, u32[]{:S(2)}, u32[]{:S(2)}) collective-permute-start(bf16[1,127,256]{1,2,0:T(8,128)(2,1)S(1)} %bitcast.99), channel_id=1, source_target_pairs={{2,0},{4,2},{6,4},{8,6},{10,8},{12,10},{14,12},{16,14},{18,16},{20... | collective-permute-start | bytes 195080 | tf_op jit(solution)/shard_map/ppermute | solution.py:12
  26.9 14.1 %reshape.453 = bf16[8192,512,1]{1,0,2:T(8,128)(2,1)} reshape(bf16[8192,2,256]{2,1,0:T(2,128)(2,1)} %param.10) | data formatting | bytes 16777216 | tf_op jit(solution)/shard_map/reshape | solution.py:98
  41.0 8.0 %copy.23 = bf16[1024,8,2,256]{3,1,2,0:T(8,128)(2,1)} copy(bf16[1024,8,2,256]{3,2,1,0:T(2,128)(2,1)} %bitcast.87) | data formatting | bytes 16777216
  49.5 2.6 %tile.10 = bf16[16,32896]{1,0:T(8,128)(2,1)} reshape(bf16[16,128,257]{2,1,0:T(8,128)(2,1)S(1)} %tile.4) | data formatting | bytes 2105344 | tf_op jit(solution)/shard_map/tile | solution.py:78
  59.1 5.1 %collective-permute-start.6 = (bf16[4,8,8192]{2,1,0:T(8,128)(2,1)S(1)}, bf16[4,8,8192]{2,1,0:T(8,128)(2,1)S(1)}, u32[]{:S(2)}, u32[]{:S(2)}) collective-permute-start(bf16[4,8,8192]{2,1,0:T(8,128)(2,1)S(1)} %broadcast_select_fusion.1), channel_id=1, source_target_pairs={{0,768},{64,832},{128,896},{192,960},{256,0},{320,64},{384,128},{4... | collective-permute-start | bytes 1572872 | tf_op jit(solution)/shard_map/ppermute | solution.py:43
  64.4 12.8 %collective-permute-done.4 = bf16[4,8,8192]{2,1,0:T(8,128)(2,1)S(1)} collective-permute-done((bf16[4,8,8192]{2,1,0:T(8,128)(2,1)S(1)}, bf16[4,8,8192]{2,1,0:T(8,128)(2,1)S(1)}, u32[]{:S(2)}, u32[]{:S(2)}) %collective-permute-start.4) | collective-permute-done | bytes 524320 | tf_op jit(solution)/shard_map/ppermute | solution.py:43
  81.5 4.9 %fusion.1 = bf16[1,128,512]{2,1,0:T(8,128)(2,1)S(1)} fusion(bf16[128,8192]{1,0:T(8,128)(2,1)S(1)} %bitcast.90, bf16[8192,512]{1,0:T(8,128)(2,1)} %bitcast.86), kind=kOutput, calls=%fused_computation.9 | convolution fusion | flops 1073807360 | bytes 10616832 | tf_op jit(solution)/shard_map/nd,dc->nc/dot_general | solution.py:101
  86.5 3.7 %collective-permute-start.13 = (bf16[1,127,256]{2,1,0:T(8,128)(2,1)S(1)}, bf16[1,127,256]{2,1,0:T(8,128)(2,1)S(1)}, u32[]{:S(2)}, u32[]{:S(2)}) collective-permute-start(bf16[1,127,256]{2,1,0:T(8,128)(2,1)S(1)} %slice.68), channel_id=1, source_target_pairs={{0,2},{2,4},{4,6},{6,8},{8,10},{10,12},{12,14},{14,16},{16,18},{18... | collective-permute-start | bytes 195080 | tf_op jit(solution)/shard_map/ppermute | solution.py:12
  90.3 2.8 %convolution_convert_fusion = bf16[4,32,8192]{2,1,0:T(8,128)(2,1)S(1)} fusion(bf16[8192,512,1]{1,0,2:T(8,128)(2,1)S(1)} %bitcast.89, bf16[4,32,256]{2,1,0:T(8,128)(2,1)S(1)} %bitcast.108, bf16[4,32,256]{2,1,0:T(8,128)(2,1)S(1)} %bitcast.107), kind=kOutput, calls=%fused_computation.2 | convolution fusion | flops 1075052544 | bytes 10616832 | tf_op jit(solution)/shard_map/bnc,dc->bnd/dot_general | solution.py:138
  95.8 4.3 %collective-permute-start.7 = (bf16[32,8192]{1,0:T(8,128)(2,1)}, bf16[32,8192]{1,0:T(8,128)(2,1)}, u32[]{:S(2)}, u32[]{:S(2)}) collective-permute-start(bf16[32,8192]{1,0:T(8,128)(2,1)} %get-tuple-element.30), channel_id=1, source_target_pairs={{0,256},{64,320},{128,384},{192,448},{256,512},{320,576},{384,640}... | collective-permute-start | bytes 1572872 | tf_op jit(solution)/shard_map/ppermute | solution.py:57
  100.1 3.6 %collective-permute-start.8 = (bf16[32,8192]{1,0:T(8,128)(2,1)}, bf16[32,8192]{1,0:T(8,128)(2,1)}, u32[]{:S(2)}, u32[]{:S(2)}) collective-permute-start(bf16[32,8192]{1,0:T(8,128)(2,1)} %get-tuple-element.32), channel_id=1, source_target_pairs={{0,512},{64,576},{128,640},{192,704},{256,768},{320,832},{384,896}... | collective-permute-start | bytes 1572872 | tf_op jit(solution)/shard_map/ppermute | solution.py:57
  103.7 3.7 %collective-permute-start.9 = (bf16[32,8192]{1,0:T(8,128)(2,1)}, bf16[32,8192]{1,0:T(8,128)(2,1)}, u32[]{:S(2)}, u32[]{:S(2)}) collective-permute-start(bf16[32,8192]{1,0:T(8,128)(2,1)} %get-tuple-element.31), channel_id=1, source_target_pairs={{0,768},{64,832},{128,896},{192,960},{256,0},{320,64},{384,128},{4... | collective-permute-start | bytes 1572872 | tf_op jit(solution)/shard_map/ppermute | solution.py:57
  109.4 3.6 %reshape.286 = f32[16,128,257]{2,1,0:T(8,128)} reshape(f32[16,32896]{1,0:T(8,128)S(1)} %pad.4) | data formatting | bytes 4210688 | tf_op jit(solution)/shard_map/reshape | solution.py:87
  118.4 3.6 %collective-permute-start.15 = (f32[16,128]{1,0:T(8,128)S(1)}, f32[16,128]{1,0:T(8,128)S(1)}, u32[]{:S(2)}, u32[]{:S(2)}) collective-permute-start(f32[16,128]{1,0:T(8,128)S(1)} %add.182), channel_id=1, source_target_pairs={{0,2},{2,0},{4,6},{6,4},{8,10},{10,8},{12,14},{14,12},{16,18},{18,... | collective-permute-start | bytes 24584 | tf_op jit(solution)/shard_map/ppermute | solution.py:21
  122.0 5.9 %collective-permute-done.15 = f32[16,128]{1,0:T(8,128)S(1)} collective-permute-done((f32[16,128]{1,0:T(8,128)S(1)}, f32[16,128]{1,0:T(8,128)S(1)}, u32[]{:S(2)}, u32[]{:S(2)}) %collective-permute-start.15) | collective-permute-done | bytes 8224 | tf_op jit(solution)/shard_map/ppermute | solution.py:21
  127.8 4.3 %collective-permute-start.16 = (f32[16,128]{1,0:T(8,128)S(1)}, f32[16,128]{1,0:T(8,128)S(1)}, u32[]{:S(2)}, u32[]{:S(2)}) collective-permute-start(f32[16,128]{1,0:T(8,128)S(1)} %add.183), channel_id=1, source_target_pairs={{0,4},{2,6},{4,0},{6,2},{8,12},{10,14},{12,8},{14,10},{16,20},{18,... | collective-permute-start | bytes 24584 | tf_op jit(solution)/shard_map/ppermute | solution.py:21
  133.7 7.3 %collective-permute-start.17 = (f32[16,128]{1,0:T(8,128)S(1)}, f32[16,128]{1,0:T(8,128)S(1)}, u32[]{:S(2)}, u32[]{:S(2)}) collective-permute-start(f32[16,128]{1,0:T(8,128)S(1)} %add.184), channel_id=1, source_target_pairs={{0,8},{2,10},{4,12},{6,14},{8,0},{10,2},{12,4},{14,6},{16,24},{18,... | collective-permute-start | bytes 24584 | tf_op jit(solution)/shard_map/ppermute | solution.py:21
  142.6 10.9 %collective-permute-start.18 = (f32[16,128]{1,0:T(8,128)S(1)}, f32[16,128]{1,0:T(8,128)S(1)}, u32[]{:S(2)}, u32[]{:S(2)}) collective-permute-start(f32[16,128]{1,0:T(8,128)S(1)} %add.185), channel_id=1, source_target_pairs={{0,16},{2,18},{4,20},{6,22},{8,24},{10,26},{12,28},{14,30},{16,0},... | collective-permute-start | bytes 24584 | tf_op jit(solution)/shard_map/ppermute | solution.py:21
  155.2 13.6 %collective-permute-start.19 = (f32[16,128]{1,0:T(8,128)S(1)}, f32[16,128]{1,0:T(8,128)S(1)}, u32[]{:S(2)}, u32[]{:S(2)}) collective-permute-start(f32[16,128]{1,0:T(8,128)S(1)} %add.186), channel_id=1, source_target_pairs={{0,32},{2,34},{4,36},{6,38},{8,40},{10,42},{12,44},{14,46},{16,48}... | collective-permute-start | bytes 24584 | tf_op jit(solution)/shard_map/ppermute | solution.py:21
  170.7 3.6 %collective-permute-start.10 = (f32[8,8192]{1,0:T(8,128)S(1)}, f32[8,8192]{1,0:T(8,128)S(1)}, u32[]{:S(2)}, u32[]{:S(2)}) collective-permute-start(f32[8,8192]{1,0:T(8,128)S(1)} %get-tuple-element.33), channel_id=1, source_target_pairs={{0,64},{64,128},{128,192},{192,0},{256,320},{320,384},{384,448},{4... | collective-permute-start | bytes 786440 | tf_op jit(solution)/shard_map/ppermute | solution.py:62
  174.3 4.0 %collective-permute-start.11 = (f32[8,8192]{1,0:T(8,128)S(1)}, f32[8,8192]{1,0:T(8,128)S(1)}, u32[]{:S(2)}, u32[]{:S(2)}) collective-permute-start(f32[8,8192]{1,0:T(8,128)S(1)} %get-tuple-element.35), channel_id=1, source_target_pairs={{0,128},{64,192},{128,0},{192,64},{256,384},{320,448},{384,256},{4... | collective-permute-start | bytes 786440 | tf_op jit(solution)/shard_map/ppermute | solution.py:62
  181.6 8.3 %collective-permute-done.10 = f32[8,8192]{1,0:T(8,128)S(1)} collective-permute-done((f32[8,8192]{1,0:T(8,128)S(1)}, f32[8,8192]{1,0:T(8,128)S(1)}, u32[]{:S(2)}, u32[]{:S(2)}) %collective-permute-start.10) | collective-permute-done | bytes 262176 | tf_op jit(solution)/shard_map/ppermute | solution.py:62
  189.9 2.8 %collective-permute-done.11 = f32[8,8192]{1,0:T(8,128)S(1)} collective-permute-done((f32[8,8192]{1,0:T(8,128)S(1)}, f32[8,8192]{1,0:T(8,128)S(1)}, u32[]{:S(2)}, u32[]{:S(2)}) %collective-permute-start.11) | collective-permute-done | bytes 262176 | tf_op jit(solution)/shard_map/ppermute | solution.py:62
  (86 shorter events, 41.5 us)
Async XLA Ops:
  0.6 53.8 %collective-permute-start.1 = (bf16[8,8192]{1,0:T(8,128)(2,1)}, bf16[8,8192]{1,0:T(8,128)(2,1)S(1)}, u32[]{:S(2)}, u32[]{:S(2)}) collective-permute-start(bf16[8,8192]{1,0:T(8,128)(2,1)} %bitcast.109), channel_id=1, source_target_pairs={{0,64},{64,128},{128,192},{192,0},{256,320},{320,384},{384,448},{4... | collective-permute-start | bytes 393224 | tf_op jit(solution)/shard_map/ppermute | solution.py:38
  3.2 51.2 %collective-permute-start.2 = (bf16[8,8192]{1,0:T(8,128)(2,1)}, bf16[8,8192]{1,0:T(8,128)(2,1)S(1)}, u32[]{:S(2)}, u32[]{:S(2)}) collective-permute-start(bf16[8,8192]{1,0:T(8,128)(2,1)} %bitcast.110), channel_id=1, source_target_pairs={{0,128},{64,192},{128,0},{192,64},{256,384},{320,448},{384,256},{4... | collective-permute-start | bytes 393224 | tf_op jit(solution)/shard_map/ppermute | solution.py:38
  8.2 46.3 %collective-permute-start.3 = (bf16[8,8192]{1,0:T(8,128)(2,1)}, bf16[8,8192]{1,0:T(8,128)(2,1)S(1)}, u32[]{:S(2)}, u32[]{:S(2)}) collective-permute-start(bf16[8,8192]{1,0:T(8,128)(2,1)} %bitcast.111), channel_id=1, source_target_pairs={{0,192},{64,0},{128,64},{192,128},{256,448},{320,256},{384,320},{4... | collective-permute-start | bytes 393224 | tf_op jit(solution)/shard_map/ppermute | solution.py:38
  12.1 41.8 %collective-permute-start = (bf16[1,127,256]{1,2,0:T(8,128)(2,1)S(1)}, bf16[1,127,256]{1,2,0:T(8,128)(2,1)S(1)}, u32[]{:S(2)}, u32[]{:S(2)}) collective-permute-start(bf16[1,127,256]{1,2,0:T(8,128)(2,1)S(1)} %bitcast.99), channel_id=1, source_target_pairs={{2,0},{4,2},{6,4},{8,6},{10,8},{12,10},{14,12},{16,14},{18,16},{20... | collective-permute-start | bytes 195080 | tf_op jit(solution)/shard_map/ppermute | solution.py:12
  41.0 8.0 %copy-start.2 = (bf16[16,128]{1,0:T(8,128)(2,1)S(1)}, bf16[16,128]{1,0:T(8,128)(2,1)}, u32[]{:S(2)}) copy-start(bf16[16,128]{1,0:T(8,128)(2,1)} %param.13) | copy-start | bytes 12292
  55.3 22.0 %collective-permute-start.4 = (bf16[4,8,8192]{2,1,0:T(8,128)(2,1)S(1)}, bf16[4,8,8192]{2,1,0:T(8,128)(2,1)S(1)}, u32[]{:S(2)}, u32[]{:S(2)}) collective-permute-start(bf16[4,8,8192]{2,1,0:T(8,128)(2,1)S(1)} %broadcast_select_fusion.1), channel_id=1, source_target_pairs={{0,256},{64,320},{128,384},{192,448},{256,512},{320,576},{384,640}... | collective-permute-start | bytes 1572872 | tf_op jit(solution)/shard_map/ppermute | solution.py:43
  57.2 20.0 %collective-permute-start.5 = (bf16[4,8,8192]{2,1,0:T(8,128)(2,1)S(1)}, bf16[4,8,8192]{2,1,0:T(8,128)(2,1)S(1)}, u32[]{:S(2)}, u32[]{:S(2)}) collective-permute-start(bf16[4,8,8192]{2,1,0:T(8,128)(2,1)S(1)} %broadcast_select_fusion.1), channel_id=1, source_target_pairs={{0,512},{64,576},{128,640},{192,704},{256,768},{320,832},{384,896}... | collective-permute-start | bytes 1572872 | tf_op jit(solution)/shard_map/ppermute | solution.py:43
  59.1 18.1 %collective-permute-start.6 = (bf16[4,8,8192]{2,1,0:T(8,128)(2,1)S(1)}, bf16[4,8,8192]{2,1,0:T(8,128)(2,1)S(1)}, u32[]{:S(2)}, u32[]{:S(2)}) collective-permute-start(bf16[4,8,8192]{2,1,0:T(8,128)(2,1)S(1)} %broadcast_select_fusion.1), channel_id=1, source_target_pairs={{0,768},{64,832},{128,896},{192,960},{256,0},{320,64},{384,128},{4... | collective-permute-start | bytes 1572872 | tf_op jit(solution)/shard_map/ppermute | solution.py:43
  79.5 10.8 %slice-start = ((s8[8388608]{0:T(1024)(128)(4,1)}), s8[4194304]{0:T(1024)(128)(4,1)S(1)}, s32[]{:S(2)}) async-start(s8[8388608]{0:T(1024)(128)(4,1)} %bitcast.88), calls=%async_computation | async-start | bytes 8388608
  81.5 8.8 %slice-start.1 = ((s8[8388608]{0:T(1024)(128)(4,1)}), s8[4194304]{0:T(1024)(128)(4,1)S(1)}, s32[]{:S(2)}) async-start(s8[8388608]{0:T(1024)(128)(4,1)} %bitcast.88), calls=%async_computation.1 | async-start | bytes 8388608
  86.5 20.8 %collective-permute-start.13 = (bf16[1,127,256]{2,1,0:T(8,128)(2,1)S(1)}, bf16[1,127,256]{2,1,0:T(8,128)(2,1)S(1)}, u32[]{:S(2)}, u32[]{:S(2)}) collective-permute-start(bf16[1,127,256]{2,1,0:T(8,128)(2,1)S(1)} %slice.68), channel_id=1, source_target_pairs={{0,2},{2,4},{4,6},{6,8},{8,10},{10,12},{12,14},{14,16},{16,18},{18... | collective-permute-start | bytes 195080 | tf_op jit(solution)/shard_map/ppermute | solution.py:12
  93.1 1.4 copy-start
  95.8 73.0 %collective-permute-start.7 = (bf16[32,8192]{1,0:T(8,128)(2,1)}, bf16[32,8192]{1,0:T(8,128)(2,1)}, u32[]{:S(2)}, u32[]{:S(2)}) collective-permute-start(bf16[32,8192]{1,0:T(8,128)(2,1)} %get-tuple-element.30), channel_id=1, source_target_pairs={{0,256},{64,320},{128,384},{192,448},{256,512},{320,576},{384,640}... | collective-permute-start | bytes 1572872 | tf_op jit(solution)/shard_map/ppermute | solution.py:57
  100.1 68.7 %collective-permute-start.8 = (bf16[32,8192]{1,0:T(8,128)(2,1)}, bf16[32,8192]{1,0:T(8,128)(2,1)}, u32[]{:S(2)}, u32[]{:S(2)}) collective-permute-start(bf16[32,8192]{1,0:T(8,128)(2,1)} %get-tuple-element.32), channel_id=1, source_target_pairs={{0,512},{64,576},{128,640},{192,704},{256,768},{320,832},{384,896}... | collective-permute-start | bytes 1572872 | tf_op jit(solution)/shard_map/ppermute | solution.py:57
  103.7 65.1 %collective-permute-start.9 = (bf16[32,8192]{1,0:T(8,128)(2,1)}, bf16[32,8192]{1,0:T(8,128)(2,1)}, u32[]{:S(2)}, u32[]{:S(2)}) collective-permute-start(bf16[32,8192]{1,0:T(8,128)(2,1)} %get-tuple-element.31), channel_id=1, source_target_pairs={{0,768},{64,832},{128,896},{192,960},{256,0},{320,64},{384,128},{4... | collective-permute-start | bytes 1572872 | tf_op jit(solution)/shard_map/ppermute | solution.py:57
  115.3 3.1 %collective-permute-start.14 = (f32[16,128]{1,0:T(8,128)S(1)}, f32[16,128]{1,0:T(8,128)S(1)}, u32[]{:S(2)}, u32[]{:S(2)}) collective-permute-start(f32[16,128]{1,0:T(8,128)S(1)} %rev.7), channel_id=1, source_target_pairs={{0,1},{1,0},{2,3},{3,2},{4,5},{5,4},{6,7},{7,6},{8,9},{9,8},{10,11... | collective-permute-start | bytes 24584 | tf_op jit(solution)/shard_map/ppermute | solution.py:21
  118.4 9.4 %collective-permute-start.15 = (f32[16,128]{1,0:T(8,128)S(1)}, f32[16,128]{1,0:T(8,128)S(1)}, u32[]{:S(2)}, u32[]{:S(2)}) collective-permute-start(f32[16,128]{1,0:T(8,128)S(1)} %add.182), channel_id=1, source_target_pairs={{0,2},{2,0},{4,6},{6,4},{8,10},{10,8},{12,14},{14,12},{16,18},{18,... | collective-permute-start | bytes 24584 | tf_op jit(solution)/shard_map/ppermute | solution.py:21
  127.8 5.9 %collective-permute-start.16 = (f32[16,128]{1,0:T(8,128)S(1)}, f32[16,128]{1,0:T(8,128)S(1)}, u32[]{:S(2)}, u32[]{:S(2)}) collective-permute-start(f32[16,128]{1,0:T(8,128)S(1)} %add.183), channel_id=1, source_target_pairs={{0,4},{2,6},{4,0},{6,2},{8,12},{10,14},{12,8},{14,10},{16,20},{18,... | collective-permute-start | bytes 24584 | tf_op jit(solution)/shard_map/ppermute | solution.py:21
  133.7 8.9 %collective-permute-start.17 = (f32[16,128]{1,0:T(8,128)S(1)}, f32[16,128]{1,0:T(8,128)S(1)}, u32[]{:S(2)}, u32[]{:S(2)}) collective-permute-start(f32[16,128]{1,0:T(8,128)S(1)} %add.184), channel_id=1, source_target_pairs={{0,8},{2,10},{4,12},{6,14},{8,0},{10,2},{12,4},{14,6},{16,24},{18,... | collective-permute-start | bytes 24584 | tf_op jit(solution)/shard_map/ppermute | solution.py:21
  142.6 12.5 %collective-permute-start.18 = (f32[16,128]{1,0:T(8,128)S(1)}, f32[16,128]{1,0:T(8,128)S(1)}, u32[]{:S(2)}, u32[]{:S(2)}) collective-permute-start(f32[16,128]{1,0:T(8,128)S(1)} %add.185), channel_id=1, source_target_pairs={{0,16},{2,18},{4,20},{6,22},{8,24},{10,26},{12,28},{14,30},{16,0},... | collective-permute-start | bytes 24584 | tf_op jit(solution)/shard_map/ppermute | solution.py:21
  155.2 25.8 %collective-permute-start.19 = (f32[16,128]{1,0:T(8,128)S(1)}, f32[16,128]{1,0:T(8,128)S(1)}, u32[]{:S(2)}, u32[]{:S(2)}) collective-permute-start(f32[16,128]{1,0:T(8,128)S(1)} %add.186), channel_id=1, source_target_pairs={{0,32},{2,34},{4,36},{6,38},{8,40},{10,42},{12,44},{14,46},{16,48}... | collective-permute-start | bytes 24584 | tf_op jit(solution)/shard_map/ppermute | solution.py:21
  170.7 19.2 %collective-permute-start.10 = (f32[8,8192]{1,0:T(8,128)S(1)}, f32[8,8192]{1,0:T(8,128)S(1)}, u32[]{:S(2)}, u32[]{:S(2)}) collective-permute-start(f32[8,8192]{1,0:T(8,128)S(1)} %get-tuple-element.33), channel_id=1, source_target_pairs={{0,64},{64,128},{128,192},{192,0},{256,320},{320,384},{384,448},{4... | collective-permute-start | bytes 786440 | tf_op jit(solution)/shard_map/ppermute | solution.py:62
  174.3 18.4 %collective-permute-start.11 = (f32[8,8192]{1,0:T(8,128)S(1)}, f32[8,8192]{1,0:T(8,128)S(1)}, u32[]{:S(2)}, u32[]{:S(2)}) collective-permute-start(f32[8,8192]{1,0:T(8,128)S(1)} %get-tuple-element.35), channel_id=1, source_target_pairs={{0,128},{64,192},{128,0},{192,64},{256,384},{320,448},{384,256},{4... | collective-permute-start | bytes 786440 | tf_op jit(solution)/shard_map/ppermute | solution.py:62
  178.3 17.0 %collective-permute-start.12 = (f32[8,8192]{1,0:T(8,128)S(1)}, f32[8,8192]{1,0:T(8,128)S(1)}, u32[]{:S(2)}, u32[]{:S(2)}) collective-permute-start(f32[8,8192]{1,0:T(8,128)S(1)} %get-tuple-element.34), channel_id=1, source_target_pairs={{0,192},{64,0},{128,64},{192,128},{256,448},{320,256},{384,320},{4... | collective-permute-start | bytes 786440 | tf_op jit(solution)/shard_map/ppermute | solution.py:62
  (2 other events, 2.1 us)

commit v3 on v2

--- a/solution.py
+++ b/solution.py
@@ -88,6 +88,15 @@
     return folded[:, tap_count:0:-1]
 
 
+def band_sums_ahead(products, tap_count):
+    groups, stretch_rows, band_width = products.shape
+    flat_view = jnp.pad(
+        products.reshape(groups, stretch_rows * band_width), ((0, 0), (0, stretch_rows))
+    )
+    folded = flat_view.reshape(groups, stretch_rows, band_width + 1).sum(axis=1)
+    return folded[:, :tap_count]
+
+
 def body(tokens, w_in, gate, cotangent, filters):
     seq_count = tokens.shape[0]
     model_width = tokens.shape[3]
@@ -99,8 +108,8 @@
     inner = 4 if lax.axis_size("tensor") % 4 == 0 else 1
     block_rows = grid_gather(tokens.reshape(tokens.shape[2], model_width), "tensor", inner)
     projected = jnp.einsum(
-        "nd,dc->nc", block_rows, weight_flat, preferred_element_type=jnp.float32
-    ).astype(jnp.bfloat16)[None]
+        "nd,djc->njc", block_rows, w_in, preferred_element_type=jnp.float32
+    ).astype(jnp.bfloat16).reshape(1, block_rows.shape[0], 2 * channels)
     second_in = projected[..., :channels].astype(jnp.float32)
     value_in = projected[..., channels:].astype(jnp.float32)
     mixed = (second_in * value_in).astype(jnp.bfloat16)
@@ -135,13 +144,24 @@
     grad_in = jnp.concatenate([grad_conv * value_in, grad_conv * second_in], axis=-1).astype(
         jnp.bfloat16
     )
-    partials = jnp.einsum("bnc,dc->bnd", grad_in, weight_flat, preferred_element_type=jnp.float32)
+    partials = jnp.einsum(
+        "bnjc,djc->bnd",
+        grad_in.reshape(grad_in.shape[:2] + (2, channels)),
+        w_in,
+        preferred_element_type=jnp.float32,
+    )
     d_tokens = grid_reduce_scatter(partials[0].astype(jnp.bfloat16), "tensor", inner)
     d_tokens = d_tokens.astype(jnp.bfloat16)[None, None]
+    grad_ahead = jnp.concatenate(
+        [grad_mix, next_rows_in, jnp.zeros((seq_count, 1, channels), jnp.bfloat16)], axis=1
+    ).reshape(seq_count, stretch_rows + tap_count, groups, group_size)
     products = jnp.einsum(
-        "btgc,bsgc->gts", grad_blocks, extended, preferred_element_type=jnp.float32
+        "bsgc,btgc->gst",
+        mixed.reshape(seq_count, stretch_rows, groups, group_size),
+        grad_ahead,
+        preferred_element_type=jnp.float32,
     )
-    local_grad = band_sums(products, tap_count)
+    local_grad = band_sums_ahead(products, tap_count)
     summed = butterfly_sum(butterfly_sum(local_grad, "dp"), "context")
     term_total = (
         seq_count * lax.axis_size("dp") * stretch_rows * lax.axis_size("context") * group_size

time: 197 us -> 184 us (0.934)
  the two profiles are of different devices: /device:TPU:40 before, /device:TPU:64 now
where the time goes in v3:
time: 184 us; the launch traced here: 183 us
  starting transfers between devices  91.1 us (50%)
  waiting for transfers between devices  50.2 us (27%)
  local copies, waits for them, and re-layouts  17.6 us (10%)
  matrix products  12.4 us (7%)
  other arithmetic  10.7 us (6%)
    ppermute x6, starting transfers between devices, butterfly_sum(): lax.ppermute(value, axis, [(i, i ^ step) for i in range(count)])  41.3 us
    ppermute x3, waiting for transfers between devices, grid_gather(): lax.ppermute(stage, axis, grid_shift(axis, s, inner, True))  21.3 us
    ppermute x3, waiting for transfers between devices, grid_reduce_scatter(): total = total + lax.ppermute(sent, axis, grid_shift(axis, s, inner, False))  12.7 us
    ppermute x6, waiting for transfers between devices, butterfly_sum(): lax.ppermute(value, axis, [(i, i ^ step) for i in range(count)])  10.8 us
    ppermute x2, starting transfers between devices, from_behind(): lax.ppermute(value, axis, [(source, source + steps) for source in range(f...  10.5 us
    ppermute x3, starting transfers between devices, grid_gather(): lax.ppermute(rows, axis, grid_shift(axis, s, inner, False))  10.3 us
    ppermute x3, starting transfers between devices, grid_gather(): lax.ppermute(stage, axis, grid_shift(axis, s, inner, True))  10.2 us
    ppermute x3, starting transfers between devices, grid_reduce_scatter(): total = total + lax.ppermute(sent, axis, grid_shift(axis, s, inner, False))  9.87 us
  transfers between devices with their start and end apart: 20, of which 10 were waited for; matrix products, arithmetic and copies ran while one was open for 8% of the time, Pallas kernels for 0%

profile of v3, /device:TPU:64, one launch (start us, length us, event | category | flops | bytes accessed | tf_op | source)
XLA Modules:
  0.0 183.4 jit_solution(11986355876179493743)
XLA Ops:
  0.6 5.5 %collective-permute-start.3 = (bf16[8,8192]{1,0:T(8,128)(2,1)}, bf16[8,8192]{1,0:T(8,128)(2,1)S(1)}, u32[]{:S(2)}, u32[]{:S(2)}) collective-permute-start(bf16[8,8192]{1,0:T(8,128)(2,1)} %bitcast.120), channel_id=1, source_target_pairs={{0,192},{64,0},{128,64},{192,128},{256,448},{320,256},{384,320},{4... | collective-permute-start | bytes 393224 | tf_op jit(solution)/shard_map/ppermute | solution.py:38
  8.1 2.9 %collective-permute-start.1 = (bf16[8,8192]{1,0:T(8,128)(2,1)}, bf16[8,8192]{1,0:T(8,128)(2,1)S(1)}, u32[]{:S(2)}, u32[]{:S(2)}) collective-permute-start(bf16[8,8192]{1,0:T(8,128)(2,1)} %bitcast.122), channel_id=1, source_target_pairs={{0,64},{64,128},{128,192},{192,0},{256,320},{320,384},{384,448},{4... | collective-permute-start | bytes 393224 | tf_op jit(solution)/shard_map/ppermute | solution.py:38
  12.9 5.0 %collective-permute-start = (bf16[1,127,256]{1,2,0:T(8,128)(2,1)S(1)}, bf16[1,127,256]{1,2,0:T(8,128)(2,1)S(1)}, u32[]{:S(2)}, u32[]{:S(2)}) collective-permute-start(bf16[1,127,256]{1,2,0:T(8,128)(2,1)S(1)} %bitcast.107), channel_id=1, source_target_pairs={{2,0},{4,2},{6,4},{8,6},{10,8},{12,10},{14,12},{16,14},{18,16},{20... | collective-permute-start | bytes 195080 | tf_op jit(solution)/shard_map/ppermute | solution.py:12
  19.5 2.6 %tile.10 = bf16[16,32896]{1,0:T(8,128)(2,1)} reshape(bf16[16,128,257]{2,1,0:T(8,128)(2,1)S(1)} %tile.4) | data formatting | bytes 2105344 | tf_op jit(solution)/shard_map/tile | solution.py:78
  25.3 4.7 %collective-permute-start.6 = (bf16[4,8,8192]{2,1,0:T(8,128)(2,1)S(1)}, bf16[4,8,8192]{2,1,0:T(8,128)(2,1)S(1)}, u32[]{:S(2)}, u32[]{:S(2)}) collective-permute-start(bf16[4,8,8192]{2,1,0:T(8,128)(2,1)S(1)} %broadcast_select_fusion), channel_id=1, source_target_pairs={{0,768},{64,832},{128,896},{192,960},{256,0},{320,64},{384,128},{4... | collective-permute-start | bytes 1572872 | tf_op jit(solution)/shard_map/ppermute | solution.py:43
  30.0 2.7 %collective-permute-start.5 = (bf16[4,8,8192]{2,1,0:T(8,128)(2,1)S(1)}, bf16[4,8,8192]{2,1,0:T(8,128)(2,1)S(1)}, u32[]{:S(2)}, u32[]{:S(2)}) collective-permute-start(bf16[4,8,8192]{2,1,0:T(8,128)(2,1)S(1)} %broadcast_select_fusion), channel_id=1, source_target_pairs={{0,512},{64,576},{128,640},{192,704},{256,768},{320,832},{384,896}... | collective-permute-start | bytes 1572872 | tf_op jit(solution)/shard_map/ppermute | solution.py:43
  32.7 2.8 %collective-permute-start.4 = (bf16[4,8,8192]{2,1,0:T(8,128)(2,1)S(1)}, bf16[4,8,8192]{2,1,0:T(8,128)(2,1)S(1)}, u32[]{:S(2)}, u32[]{:S(2)}) collective-permute-start(bf16[4,8,8192]{2,1,0:T(8,128)(2,1)S(1)} %broadcast_select_fusion), channel_id=1, source_target_pairs={{0,256},{64,320},{128,384},{192,448},{256,512},{320,576},{384,640}... | collective-permute-start | bytes 1572872 | tf_op jit(solution)/shard_map/ppermute | solution.py:43
  35.6 15.7 %collective-permute-done.6 = bf16[4,8,8192]{2,1,0:T(8,128)(2,1)S(1)} collective-permute-done((bf16[4,8,8192]{2,1,0:T(8,128)(2,1)S(1)}, bf16[4,8,8192]{2,1,0:T(8,128)(2,1)S(1)}, u32[]{:S(2)}, u32[]{:S(2)}) %collective-permute-start.6) | collective-permute-done | bytes 524320 | tf_op jit(solution)/shard_map/ppermute | solution.py:43
  51.3 5.6 %collective-permute-done.4 = bf16[4,8,8192]{2,1,0:T(8,128)(2,1)S(1)} collective-permute-done((bf16[4,8,8192]{2,1,0:T(8,128)(2,1)S(1)}, bf16[4,8,8192]{2,1,0:T(8,128)(2,1)S(1)}, u32[]{:S(2)}, u32[]{:S(2)}) %collective-permute-start.4) | collective-permute-done | bytes 524320 | tf_op jit(solution)/shard_map/ppermute | solution.py:43
  61.0 4.7 %fusion.5 = bf16[128,2,256]{2,0,1:T(8,128)(2,1)S(1)} fusion(bf16[8192,2,256]{2,1,0:T(2,128)(2,1)} %param.10, bf16[128,8192]{1,0:T(8,128)(2,1)S(1)} %bitcast_select_fusion), kind=kOutput, calls=%fused_computation.11 | convolution fusion | flops 1073807360 | bytes 10616832 | tf_op jit(solution)/shard_map/nd,djc->njc/dot_general | solution.py:110
  68.8 3.6 %reshape.296 = f32[16,128,257]{2,1,0:T(8,128)} reshape(f32[16,32896]{1,0:T(8,128)S(1)} %pad.4) | data formatting | bytes 4210688 | tf_op jit(solution)/shard_map/reshape | solution.py:96
  76.5 6.3 %fusion = bf16[128,8192]{1,0:T(8,128)(2,1)S(1)} fusion(bf16[8192,2,256]{2,1,0:T(2,128)(2,1)} %param.10, bf16[128,1,256]{2,0,1:T(8,128)(2,1)S(1)} %copy-done.3, bf16[128,1,256]{2,0,1:T(8,128)(2,1)S(1)} %copy-done.2), kind=kOutput, calls=%fused_computation.3 | convolution fusion | flops 1074855936 | bytes 10616832 | tf_op jit(solution)/shard_map/bnjc,djc->bnd/dot_general | solution.py:147
  86.2 5.1 %collective-permute-start.9 = (bf16[32,8192]{1,0:T(8,128)(2,1)S(1)}, bf16[32,8192]{1,0:T(8,128)(2,1)}, u32[]{:S(2)}, u32[]{:S(2)}) collective-permute-start(bf16[32,8192]{1,0:T(8,128)(2,1)S(1)} %get-tuple-element.31), channel_id=1, source_target_pairs={{0,768},{64,832},{128,896},{192,960},{256,0},{320,64},{384,128},{4... | collective-permute-start | bytes 1572872 | tf_op jit(solution)/shard_map/ppermute | solution.py:57
  93.3 5.5 %collective-permute-start.15 = (f32[16,128]{1,0:T(8,128)S(1)}, f32[16,128]{1,0:T(8,128)S(1)}, u32[]{:S(2)}, u32[]{:S(2)}) collective-permute-start(f32[16,128]{1,0:T(8,128)S(1)} %slice_add_fusion), channel_id=1, source_target_pairs={{0,2},{2,0},{4,6},{6,4},{8,10},{10,8},{12,14},{14,12},{16,18},{18,... | collective-permute-start | bytes 24584 | tf_op jit(solution)/shard_map/ppermute | solution.py:21
  98.8 3.9 %collective-permute-done.15 = f32[16,128]{1,0:T(8,128)S(1)} collective-permute-done((f32[16,128]{1,0:T(8,128)S(1)}, f32[16,128]{1,0:T(8,128)S(1)}, u32[]{:S(2)}, u32[]{:S(2)}) %collective-permute-start.15) | collective-permute-done | bytes 8224 | tf_op jit(solution)/shard_map/ppermute | solution.py:21
  104.7 3.6 %collective-permute-done.16 = f32[16,128]{1,0:T(8,128)S(1)} collective-permute-done((f32[16,128]{1,0:T(8,128)S(1)}, f32[16,128]{1,0:T(8,128)S(1)}, u32[]{:S(2)}, u32[]{:S(2)}) %collective-permute-start.16) | collective-permute-done | bytes 8224 | tf_op jit(solution)/shard_map/ppermute | solution.py:21
  108.3 6.1 %collective-permute-start.17 = (f32[16,128]{1,0:T(8,128)S(1)}, f32[16,128]{1,0:T(8,128)S(1)}, u32[]{:S(2)}, u32[]{:S(2)}) collective-permute-start(f32[16,128]{1,0:T(8,128)S(1)} %add.184), channel_id=1, source_target_pairs={{0,8},{2,10},{4,12},{6,14},{8,0},{10,2},{12,4},{14,6},{16,24},{18,... | collective-permute-start | bytes 24584 | tf_op jit(solution)/shard_map/ppermute | solution.py:21
  116.0 10.9 %collective-permute-start.18 = (f32[16,128]{1,0:T(8,128)S(1)}, f32[16,128]{1,0:T(8,128)S(1)}, u32[]{:S(2)}, u32[]{:S(2)}) collective-permute-start(f32[16,128]{1,0:T(8,128)S(1)} %add.185), channel_id=1, source_target_pairs={{0,16},{2,18},{4,20},{6,22},{8,24},{10,26},{12,28},{14,30},{16,0},... | collective-permute-start | bytes 24584 | tf_op jit(solution)/shard_map/ppermute | solution.py:21
  128.5 15.0 %collective-permute-start.19 = (f32[16,128]{1,0:T(8,128)S(1)}, f32[16,128]{1,0:T(8,128)S(1)}, u32[]{:S(2)}, u32[]{:S(2)}) collective-permute-start(f32[16,128]{1,0:T(8,128)S(1)} %add.186), channel_id=1, source_target_pairs={{0,32},{2,34},{4,36},{6,38},{8,40},{10,42},{12,44},{14,46},{16,48}... | collective-permute-start | bytes 24584 | tf_op jit(solution)/shard_map/ppermute | solution.py:21
  143.7 5.4 %collective-permute-start.13 = (bf16[1,127,256]{2,1,0:T(8,128)(2,1)S(1)}, bf16[1,127,256]{2,1,0:T(8,128)(2,1)S(1)}, u32[]{:S(2)}, u32[]{:S(2)}) collective-permute-start(bf16[1,127,256]{2,1,0:T(8,128)(2,1)S(1)} %slice.68), channel_id=1, source_target_pairs={{0,2},{2,4},{4,6},{6,8},{8,10},{10,12},{12,14},{14,16},{16,18},{18... | collective-permute-start | bytes 195080 | tf_op jit(solution)/shard_map/ppermute | solution.py:12
  149.7 5.4 %collective-permute-done.13 = bf16[1,127,256]{2,1,0:T(8,128)(2,1)S(1)} collective-permute-done((bf16[1,127,256]{2,1,0:T(8,128)(2,1)S(1)}, bf16[1,127,256]{2,1,0:T(8,128)(2,1)S(1)}, u32[]{:S(2)}, u32[]{:S(2)}) %collective-permute-start.13) | collective-permute-done | bytes 65056 | tf_op jit(solution)/shard_map/ppermute | solution.py:12
  158.0 3.0 %collective-permute-start.10 = (f32[8,8192]{1,0:T(8,128)}, f32[8,8192]{1,0:T(8,128)S(1)}, u32[]{:S(2)}, u32[]{:S(2)}) collective-permute-start(f32[8,8192]{1,0:T(8,128)} %get-tuple-element.33), channel_id=1, source_target_pairs={{0,64},{64,128},{128,192},{192,0},{256,320},{320,384},{384,448},{4... | collective-permute-start | bytes 786440 | tf_op jit(solution)/shard_map/ppermute | solution.py:62
  161.0 4.6 %collective-permute-start.12 = (f32[8,8192]{1,0:T(8,128)S(1)}, f32[8,8192]{1,0:T(8,128)S(1)}, u32[]{:S(2)}, u32[]{:S(2)}) collective-permute-start(f32[8,8192]{1,0:T(8,128)S(1)} %get-tuple-element.34), channel_id=1, source_target_pairs={{0,192},{64,0},{128,64},{192,128},{256,448},{320,256},{384,320},{4... | collective-permute-start | bytes 786440 | tf_op jit(solution)/shard_map/ppermute | solution.py:62
  172.7 9.1 %collective-permute-done.11 = f32[8,8192]{1,0:T(8,128)} collective-permute-done((f32[8,8192]{1,0:T(8,128)S(1)}, f32[8,8192]{1,0:T(8,128)}, u32[]{:S(2)}, u32[]{:S(2)}) %collective-permute-start.11) | collective-permute-done | bytes 262176 | tf_op jit(solution)/shard_map/ppermute | solution.py:62
  (88 shorter events, 42.2 us)
Async XLA Ops:
  0.6 23.8 %collective-permute-start.3 = (bf16[8,8192]{1,0:T(8,128)(2,1)}, bf16[8,8192]{1,0:T(8,128)(2,1)S(1)}, u32[]{:S(2)}, u32[]{:S(2)}) collective-permute-start(bf16[8,8192]{1,0:T(8,128)(2,1)} %bitcast.120), channel_id=1, source_target_pairs={{0,192},{64,0},{128,64},{192,128},{256,448},{320,256},{384,320},{4... | collective-permute-start | bytes 393224 | tf_op jit(solution)/shard_map/ppermute | solution.py:38
  6.1 18.3 %collective-permute-start.2 = (bf16[8,8192]{1,0:T(8,128)(2,1)}, bf16[8,8192]{1,0:T(8,128)(2,1)S(1)}, u32[]{:S(2)}, u32[]{:S(2)}) collective-permute-start(bf16[8,8192]{1,0:T(8,128)(2,1)} %bitcast.121), channel_id=1, source_target_pairs={{0,128},{64,192},{128,0},{192,64},{256,384},{320,448},{384,256},{4... | collective-permute-start | bytes 393224 | tf_op jit(solution)/shard_map/ppermute | solution.py:38
  8.1 16.4 %collective-permute-start.1 = (bf16[8,8192]{1,0:T(8,128)(2,1)}, bf16[8,8192]{1,0:T(8,128)(2,1)S(1)}, u32[]{:S(2)}, u32[]{:S(2)}) collective-permute-start(bf16[8,8192]{1,0:T(8,128)(2,1)} %bitcast.122), channel_id=1, source_target_pairs={{0,64},{64,128},{128,192},{192,0},{256,320},{320,384},{384,448},{4... | collective-permute-start | bytes 393224 | tf_op jit(solution)/shard_map/ppermute | solution.py:38
  12.9 11.0 %collective-permute-start = (bf16[1,127,256]{1,2,0:T(8,128)(2,1)S(1)}, bf16[1,127,256]{1,2,0:T(8,128)(2,1)S(1)}, u32[]{:S(2)}, u32[]{:S(2)}) collective-permute-start(bf16[1,127,256]{1,2,0:T(8,128)(2,1)S(1)} %bitcast.107), channel_id=1, source_target_pairs={{2,0},{4,2},{6,4},{8,6},{10,8},{12,10},{14,12},{16,14},{18,16},{20... | collective-permute-start | bytes 195080 | tf_op jit(solution)/shard_map/ppermute | solution.py:12
  22.1 1.2 slice-start
  25.3 26.0 %collective-permute-start.6 = (bf16[4,8,8192]{2,1,0:T(8,128)(2,1)S(1)}, bf16[4,8,8192]{2,1,0:T(8,128)(2,1)S(1)}, u32[]{:S(2)}, u32[]{:S(2)}) collective-permute-start(bf16[4,8,8192]{2,1,0:T(8,128)(2,1)S(1)} %broadcast_select_fusion), channel_id=1, source_target_pairs={{0,768},{64,832},{128,896},{192,960},{256,0},{320,64},{384,128},{4... | collective-permute-start | bytes 1572872 | tf_op jit(solution)/shard_map/ppermute | solution.py:43
  30.0 21.3 %collective-permute-start.5 = (bf16[4,8,8192]{2,1,0:T(8,128)(2,1)S(1)}, bf16[4,8,8192]{2,1,0:T(8,128)(2,1)S(1)}, u32[]{:S(2)}, u32[]{:S(2)}) collective-permute-start(bf16[4,8,8192]{2,1,0:T(8,128)(2,1)S(1)} %broadcast_select_fusion), channel_id=1, source_target_pairs={{0,512},{64,576},{128,640},{192,704},{256,768},{320,832},{384,896}... | collective-permute-start | bytes 1572872 | tf_op jit(solution)/shard_map/ppermute | solution.py:43
  32.7 24.2 %collective-permute-start.4 = (bf16[4,8,8192]{2,1,0:T(8,128)(2,1)S(1)}, bf16[4,8,8192]{2,1,0:T(8,128)(2,1)S(1)}, u32[]{:S(2)}, u32[]{:S(2)}) collective-permute-start(bf16[4,8,8192]{2,1,0:T(8,128)(2,1)S(1)} %broadcast_select_fusion), channel_id=1, source_target_pairs={{0,256},{64,320},{128,384},{192,448},{256,512},{320,576},{384,640}... | collective-permute-start | bytes 1572872 | tf_op jit(solution)/shard_map/ppermute | solution.py:43
  72.4 4.1 %copy-start.2 = (bf16[128,1,256]{2,0,1:T(8,128)(2,1)S(1)}, bf16[128,1,256]{2,0,1:T(8,128)(2,1)}, u32[]{:S(2)}) copy-start(bf16[128,1,256]{2,0,1:T(8,128)(2,1)} %get-tuple-element.36) | copy-start | bytes 196612
  72.4 4.1 %copy-start.3 = (bf16[128,1,256]{2,0,1:T(8,128)(2,1)S(1)}, bf16[128,1,256]{2,0,1:T(8,128)(2,1)}, u32[]{:S(2)}) copy-start(bf16[128,1,256]{2,0,1:T(8,128)(2,1)} %get-tuple-element.37) | copy-start | bytes 196612
  74.6 18.7 %collective-permute-start.14 = (f32[16,128]{1,0:T(8,128)S(1)}, f32[16,128]{1,0:T(8,128)S(1)}, u32[]{:S(2)}, u32[]{:S(2)}) collective-permute-start(f32[16,128]{1,0:T(8,128)S(1)} %slice.69), channel_id=1, source_target_pairs={{0,1},{1,0},{2,3},{3,2},{4,5},{5,4},{6,7},{7,6},{8,9},{9,8},{10,11... | collective-permute-start | bytes 24584 | tf_op jit(solution)/shard_map/ppermute | solution.py:21
  82.8 1.3 copy-start
  84.3 71.1 %collective-permute-start.7 = (bf16[32,8192]{1,0:T(8,128)(2,1)S(1)}, bf16[32,8192]{1,0:T(8,128)(2,1)}, u32[]{:S(2)}, u32[]{:S(2)}) collective-permute-start(bf16[32,8192]{1,0:T(8,128)(2,1)S(1)} %get-tuple-element.30), channel_id=1, source_target_pairs={{0,256},{64,320},{128,384},{192,448},{256,512},{320,576},{384,640}... | collective-permute-start | bytes 1572872 | tf_op jit(solution)/shard_map/ppermute | solution.py:57
  86.2 69.1 %collective-permute-start.9 = (bf16[32,8192]{1,0:T(8,128)(2,1)S(1)}, bf16[32,8192]{1,0:T(8,128)(2,1)}, u32[]{:S(2)}, u32[]{:S(2)}) collective-permute-start(bf16[32,8192]{1,0:T(8,128)(2,1)S(1)} %get-tuple-element.31), channel_id=1, source_target_pairs={{0,768},{64,832},{128,896},{192,960},{256,0},{320,64},{384,128},{4... | collective-permute-start | bytes 1572872 | tf_op jit(solution)/shard_map/ppermute | solution.py:57
  91.4 64.0 %collective-permute-start.8 = (bf16[32,8192]{1,0:T(8,128)(2,1)S(1)}, bf16[32,8192]{1,0:T(8,128)(2,1)}, u32[]{:S(2)}, u32[]{:S(2)}) collective-permute-start(bf16[32,8192]{1,0:T(8,128)(2,1)S(1)} %get-tuple-element.32), channel_id=1, source_target_pairs={{0,512},{64,576},{128,640},{192,704},{256,768},{320,832},{384,896}... | collective-permute-start | bytes 1572872 | tf_op jit(solution)/shard_map/ppermute | solution.py:57
  93.3 9.5 %collective-permute-start.15 = (f32[16,128]{1,0:T(8,128)S(1)}, f32[16,128]{1,0:T(8,128)S(1)}, u32[]{:S(2)}, u32[]{:S(2)}) collective-permute-start(f32[16,128]{1,0:T(8,128)S(1)} %slice_add_fusion), channel_id=1, source_target_pairs={{0,2},{2,0},{4,6},{6,4},{8,10},{10,8},{12,14},{14,12},{16,18},{18,... | collective-permute-start | bytes 24584 | tf_op jit(solution)/shard_map/ppermute | solution.py:21
  102.8 5.5 %collective-permute-start.16 = (f32[16,128]{1,0:T(8,128)S(1)}, f32[16,128]{1,0:T(8,128)S(1)}, u32[]{:S(2)}, u32[]{:S(2)}) collective-permute-start(f32[16,128]{1,0:T(8,128)S(1)} %add.183), channel_id=1, source_target_pairs={{0,4},{2,6},{4,0},{6,2},{8,12},{10,14},{12,8},{14,10},{16,20},{18,... | collective-permute-start | bytes 24584 | tf_op jit(solution)/shard_map/ppermute | solution.py:21
  108.3 7.7 %collective-permute-start.17 = (f32[16,128]{1,0:T(8,128)S(1)}, f32[16,128]{1,0:T(8,128)S(1)}, u32[]{:S(2)}, u32[]{:S(2)}) collective-permute-start(f32[16,128]{1,0:T(8,128)S(1)} %add.184), channel_id=1, source_target_pairs={{0,8},{2,10},{4,12},{6,14},{8,0},{10,2},{12,4},{14,6},{16,24},{18,... | collective-permute-start | bytes 24584 | tf_op jit(solution)/shard_map/ppermute | solution.py:21
  116.0 12.5 %collective-permute-start.18 = (f32[16,128]{1,0:T(8,128)S(1)}, f32[16,128]{1,0:T(8,128)S(1)}, u32[]{:S(2)}, u32[]{:S(2)}) collective-permute-start(f32[16,128]{1,0:T(8,128)S(1)} %add.185), channel_id=1, source_target_pairs={{0,16},{2,18},{4,20},{6,22},{8,24},{10,26},{12,28},{14,30},{16,0},... | collective-permute-start | bytes 24584 | tf_op jit(solution)/shard_map/ppermute | solution.py:21
  128.5 20.6 %collective-permute-start.19 = (f32[16,128]{1,0:T(8,128)S(1)}, f32[16,128]{1,0:T(8,128)S(1)}, u32[]{:S(2)}, u32[]{:S(2)}) collective-permute-start(f32[16,128]{1,0:T(8,128)S(1)} %add.186), channel_id=1, source_target_pairs={{0,32},{2,34},{4,36},{6,38},{8,40},{10,42},{12,44},{14,46},{16,48}... | collective-permute-start | bytes 24584 | tf_op jit(solution)/shard_map/ppermute | solution.py:21
  143.7 11.4 %collective-permute-start.13 = (bf16[1,127,256]{2,1,0:T(8,128)(2,1)S(1)}, bf16[1,127,256]{2,1,0:T(8,128)(2,1)S(1)}, u32[]{:S(2)}, u32[]{:S(2)}) collective-permute-start(bf16[1,127,256]{2,1,0:T(8,128)(2,1)S(1)} %slice.68), channel_id=1, source_target_pairs={{0,2},{2,4},{4,6},{6,8},{8,10},{10,12},{12,14},{14,16},{16,18},{18... | collective-permute-start | bytes 195080 | tf_op jit(solution)/shard_map/ppermute | solution.py:12
  158.0 12.6 %collective-permute-start.10 = (f32[8,8192]{1,0:T(8,128)}, f32[8,8192]{1,0:T(8,128)S(1)}, u32[]{:S(2)}, u32[]{:S(2)}) collective-permute-start(f32[8,8192]{1,0:T(8,128)} %get-tuple-element.33), channel_id=1, source_target_pairs={{0,64},{64,128},{128,192},{192,0},{256,320},{320,384},{384,448},{4... | collective-permute-start | bytes 786440 | tf_op jit(solution)/shard_map/ppermute | solution.py:62
  161.0 11.7 %collective-permute-start.12 = (f32[8,8192]{1,0:T(8,128)S(1)}, f32[8,8192]{1,0:T(8,128)S(1)}, u32[]{:S(2)}, u32[]{:S(2)}) collective-permute-start(f32[8,8192]{1,0:T(8,128)S(1)} %get-tuple-element.34), channel_id=1, source_target_pairs={{0,192},{64,0},{128,64},{192,128},{256,448},{320,256},{384,320},{4... | collective-permute-start | bytes 786440 | tf_op jit(solution)/shard_map/ppermute | solution.py:62
  165.6 16.1 %collective-permute-start.11 = (f32[8,8192]{1,0:T(8,128)S(1)}, f32[8,8192]{1,0:T(8,128)}, u32[]{:S(2)}, u32[]{:S(2)}) collective-permute-start(f32[8,8192]{1,0:T(8,128)S(1)} %get-tuple-element.35), channel_id=1, source_target_pairs={{0,128},{64,192},{128,0},{192,64},{256,384},{320,448},{384,256},{4... | collective-permute-start | bytes 786440 | tf_op jit(solution)/shard_map/ppermute | solution.py:62
  (1 other events, 0.9 us)

commit v4 on v3

--- a/solution.py
+++ b/solution.py
@@ -20,6 +20,13 @@
     while step < count:
         value = value + lax.ppermute(value, axis, [(i, i ^ step) for i in range(count)])
         step *= 2
+    return value
+
+
+def butterfly_rounds(value, axis, steps):
+    count = lax.axis_size(axis)
+    for step in steps:
+        value = value + lax.ppermute(value, axis, [(i, i ^ step) for i in range(count)])
     return value
 
 
@@ -46,21 +53,18 @@
     return jnp.take(jnp.stack(pieces), order, axis=0).reshape((count * rows.shape[0],) + rows.shape[1:])
 
 
-def grid_reduce_scatter(partial_rows, axis, inner):
-    count = lax.axis_size(axis)
-    outer = count // inner
+def scatter_stage(chunks, axis, inner, outer_step, wide):
+    count = lax.axis_size(axis)
+    size = count // inner if outer_step else inner
     index = lax.axis_index(axis)
-    chunks = partial_rows.reshape((outer, -1) + partial_rows.shape[1:])
-    acc = jnp.take(chunks, index // inner, axis=0).astype(jnp.float32)
-    for s in range(1, outer):
-        sent = jnp.take(chunks, (index // inner + s) % outer, axis=0)
-        acc = acc + lax.ppermute(sent, axis, grid_shift(axis, s, inner, True)).astype(jnp.float32)
-    chunks = acc.reshape((inner, -1) + acc.shape[1:])
-    total = jnp.take(chunks, index % inner, axis=0)
-    for s in range(1, inner):
-        sent = jnp.take(chunks, (index % inner + s) % inner, axis=0)
-        total = total + lax.ppermute(sent, axis, grid_shift(axis, s, inner, False))
-    return total
+    place = index // inner if outer_step else index % inner
+    acc = jnp.take(chunks, place, axis=0).astype(jnp.float32)
+    for s in range(1, size):
+        sent = jnp.take(chunks, (place + s) % size, axis=0)
+        if wide:
+            sent = sent.astype(jnp.float32)
+        acc = acc + lax.ppermute(sent, axis, grid_shift(axis, s, inner, outer_step)).astype(jnp.float32)
+    return acc
 
 
 def skew_band(filters, stretch_rows):
@@ -150,8 +154,9 @@
         w_in,
         preferred_element_type=jnp.float32,
     )
-    d_tokens = grid_reduce_scatter(partials[0].astype(jnp.bfloat16), "tensor", inner)
-    d_tokens = d_tokens.astype(jnp.bfloat16)[None, None]
+    outer = lax.axis_size("tensor") // inner
+    partial_rows = partials[0].astype(jnp.bfloat16)
+    x_chunks = partial_rows.reshape((outer, -1) + partial_rows.shape[1:])
     grad_ahead = jnp.concatenate(
         [grad_mix, next_rows_in, jnp.zeros((seq_count, 1, channels), jnp.bfloat16)], axis=1
     ).reshape(seq_count, stretch_rows + tap_count, groups, group_size)
@@ -162,7 +167,22 @@
         preferred_element_type=jnp.float32,
     )
     local_grad = band_sums_ahead(products, tap_count)
-    summed = butterfly_sum(butterfly_sum(local_grad, "dp"), "context")
+    if lax.axis_size("context") & (lax.axis_size("context") - 1) or lax.axis_size("dp") & (lax.axis_size("dp") - 1):
+        summed = lax.psum(local_grad, ("context", "dp"))
+        x_sums = scatter_stage(x_chunks, "tensor", inner, True, False)
+        d_tokens = scatter_stage(x_sums.reshape((inner, -1) + x_sums.shape[1:]), "tensor", inner, False, True)
+    else:
+        context_steps = [1 << k for k in range(lax.axis_size("context").bit_length() - 1)]
+        dp_steps = [1 << k for k in range(lax.axis_size("dp").bit_length() - 1)]
+        first, second, third = context_steps[:1], context_steps[1:3], context_steps[3:]
+        summed = butterfly_rounds(butterfly_rounds(local_grad, "dp", dp_steps), "context", first)
+        x_sums = scatter_stage(x_chunks, "tensor", inner, True, False)
+        x_sums, summed = lax.optimization_barrier((x_sums, summed))
+        summed = butterfly_rounds(summed, "context", second)
+        d_tokens = scatter_stage(x_sums.reshape((inner, -1) + x_sums.shape[1:]), "tensor", inner, False, True)
+        d_tokens, summed = lax.optimization_barrier((d_tokens, summed))
+        summed = butterfly_rounds(summed, "context", third)
+    d_tokens = d_tokens.astype(jnp.bfloat16)[None, None]
     term_total = (
         seq_count * lax.axis_size("dp") * stretch_rows * lax.axis_size("context") * group_size
     )

time: 184 us -> 169 us (0.918)
  the two profiles are of different devices: /device:TPU:64 before, /device:TPU:1 now
where the time goes in v4:
time: 169 us; the launch traced here: 167 us
  starting transfers between devices  99.9 us (59%)
  waiting for transfers between devices  24.9 us (15%)
  local copies, waits for them, and re-layouts  16.2 us (10%)
  matrix products  12.4 us (7%)
  other arithmetic  11.7 us (7%)
    ppermute x6, starting transfers between devices, butterfly_rounds(): lax.ppermute(value, axis, [(i, i ^ step) for i in range(count)])  57.3 us
    ppermute x6, starting transfers between devices, scatter_stage(): lax.ppermute(sent, axis, grid_shift(axis, s, inner, outer_step))  19.4 us
    ppermute x3, waiting for transfers between devices, grid_gather(): lax.ppermute(stage, axis, grid_shift(axis, s, inner, True))  12.9 us
    ppermute x3, starting transfers between devices, grid_gather(): lax.ppermute(rows, axis, grid_shift(axis, s, inner, False))  10.3 us
    ppermute x3, starting transfers between devices, grid_gather(): lax.ppermute(stage, axis, grid_shift(axis, s, inner, True))  9.33 us
    dot_general x1, matrix products, body(): jnp.einsum('bnjc,djc->bnd', grad_in.reshape(grad_in.shape[:2] + (2, chann...  6.27 us
    unnamed x11, local copies, waits for them, and re-layouts  5.7 us
    ppermute x6, waiting for transfers between devices, scatter_stage(): lax.ppermute(sent, axis, grid_shift(axis, s, inner, outer_step))  5.38 us
  transfers between devices with their start and end apart: 20, of which 9 were waited for; matrix products, arithmetic and copies ran while one was open for 12% of the time, Pallas kernels for 0%

profile of v4, /device:TPU:1, one launch (start us, length us, event | category | flops | bytes accessed | tf_op | source)
XLA Modules:
  0.0 166.6 jit_solution(6882709992105258509)
XLA Ops:
  0.6 6.0 %collective-permute-start.3 = (bf16[8,8192]{1,0:T(8,128)(2,1)}, bf16[8,8192]{1,0:T(8,128)(2,1)S(1)}, u32[]{:S(2)}, u32[]{:S(2)}) collective-permute-start(bf16[8,8192]{1,0:T(8,128)(2,1)} %bitcast.118), channel_id=1, source_target_pairs={{0,192},{64,0},{128,64},{192,128},{256,448},{320,256},{384,320},{4... | collective-permute-start | bytes 393224 | tf_op jit(solution)/shard_map/ppermute | solution.py:45
  8.6 2.4 %collective-permute-start.1 = (bf16[8,8192]{1,0:T(8,128)(2,1)}, bf16[8,8192]{1,0:T(8,128)(2,1)S(1)}, u32[]{:S(2)}, u32[]{:S(2)}) collective-permute-start(bf16[8,8192]{1,0:T(8,128)(2,1)} %bitcast.120), channel_id=1, source_target_pairs={{0,64},{64,128},{128,192},{192,0},{256,320},{320,384},{384,448},{4... | collective-permute-start | bytes 393224 | tf_op jit(solution)/shard_map/ppermute | solution.py:45
  18.1 3.8 %collective-permute-done = bf16[1,127,256]{1,2,0:T(8,128)(2,1)S(1)} collective-permute-done((bf16[1,127,256]{1,2,0:T(8,128)(2,1)S(1)}, bf16[1,127,256]{1,2,0:T(8,128)(2,1)S(1)}, u32[]{:S(2)}, u32[]{:S(2)}) %collective-permute-start) | collective-permute-done | bytes 65056 | tf_op jit(solution)/shard_map/ppermute | solution.py:12
  23.3 4.4 %collective-permute-start.6 = (bf16[4,8,8192]{2,1,0:T(8,128)(2,1)S(1)}, bf16[4,8,8192]{2,1,0:T(8,128)(2,1)S(1)}, u32[]{:S(2)}, u32[]{:S(2)}) collective-permute-start(bf16[4,8,8192]{2,1,0:T(8,128)(2,1)S(1)} %broadcast_select_fusion), channel_id=1, source_target_pairs={{0,768},{64,832},{128,896},{192,960},{256,0},{320,64},{384,128},{4... | collective-permute-start | bytes 1572872 | tf_op jit(solution)/shard_map/ppermute | solution.py:50
  27.7 2.4 %collective-permute-start.5 = (bf16[4,8,8192]{2,1,0:T(8,128)(2,1)S(1)}, bf16[4,8,8192]{2,1,0:T(8,128)(2,1)S(1)}, u32[]{:S(2)}, u32[]{:S(2)}) collective-permute-start(bf16[4,8,8192]{2,1,0:T(8,128)(2,1)S(1)} %broadcast_select_fusion), channel_id=1, source_target_pairs={{0,512},{64,576},{128,640},{192,704},{256,768},{320,832},{384,896}... | collective-permute-start | bytes 1572872 | tf_op jit(solution)/shard_map/ppermute | solution.py:50
  30.2 2.5 %collective-permute-start.4 = (bf16[4,8,8192]{2,1,0:T(8,128)(2,1)S(1)}, bf16[4,8,8192]{2,1,0:T(8,128)(2,1)S(1)}, u32[]{:S(2)}, u32[]{:S(2)}) collective-permute-start(bf16[4,8,8192]{2,1,0:T(8,128)(2,1)S(1)} %broadcast_select_fusion), channel_id=1, source_target_pairs={{0,256},{64,320},{128,384},{192,448},{256,512},{320,576},{384,640}... | collective-permute-start | bytes 1572872 | tf_op jit(solution)/shard_map/ppermute | solution.py:50
  32.8 7.5 %collective-permute-done.6 = bf16[4,8,8192]{2,1,0:T(8,128)(2,1)S(1)} collective-permute-done((bf16[4,8,8192]{2,1,0:T(8,128)(2,1)S(1)}, bf16[4,8,8192]{2,1,0:T(8,128)(2,1)S(1)}, u32[]{:S(2)}, u32[]{:S(2)}) %collective-permute-start.6) | collective-permute-done | bytes 524320 | tf_op jit(solution)/shard_map/ppermute | solution.py:50
  40.3 5.3 %collective-permute-done.4 = bf16[4,8,8192]{2,1,0:T(8,128)(2,1)S(1)} collective-permute-done((bf16[4,8,8192]{2,1,0:T(8,128)(2,1)S(1)}, bf16[4,8,8192]{2,1,0:T(8,128)(2,1)S(1)}, u32[]{:S(2)}, u32[]{:S(2)}) %collective-permute-start.4) | collective-permute-done | bytes 524320 | tf_op jit(solution)/shard_map/ppermute | solution.py:50
  49.8 4.7 %fusion.5 = bf16[128,2,256]{2,0,1:T(8,128)(2,1)S(1)} fusion(bf16[8192,2,256]{2,1,0:T(2,128)(2,1)} %param.10, bf16[128,8192]{1,0:T(8,128)(2,1)S(1)} %bitcast_select_fusion), kind=kOutput, calls=%fused_computation.11 | convolution fusion | flops 1073807360 | bytes 10616832 | tf_op jit(solution)/shard_map/nd,djc->njc/dot_general | solution.py:114
  54.9 6.3 %fusion = bf16[128,8192]{1,0:T(8,128)(2,1)S(1)} fusion(bf16[8192,2,256]{2,1,0:T(2,128)(2,1)} %param.10, bf16[128,1,256]{2,0,1:T(8,128)(2,1)S(1)} %get-tuple-element.45, bf16[128,1,256]{2,0,1:T(8,128)(2,1)S(1)} %get-tuple-element.44), kind=kOutput, calls=%fused_computation.3 | convolution fusion | flops 1074855936 | bytes 10616832 | tf_op jit(solution)/shard_map/bnjc,djc->bnd/dot_general | solution.py:151
  63.8 3.9 %collective-permute-start.7 = (bf16[32,8192]{1,0:T(8,128)(2,1)}, bf16[32,8192]{1,0:T(8,128)(2,1)}, u32[]{:S(2)}, u32[]{:S(2)}) collective-permute-start(bf16[32,8192]{1,0:T(8,128)(2,1)} %get-tuple-element.38), channel_id=1, source_target_pairs={{0,256},{64,320},{128,384},{192,448},{256,512},{320,576},{384,640}... | collective-permute-start | bytes 1572872 | tf_op jit(solution)/shard_map/ppermute | solution.py:66
  67.7 2.6 %collective-permute-start.9 = (bf16[32,8192]{1,0:T(8,128)(2,1)}, bf16[32,8192]{1,0:T(8,128)(2,1)}, u32[]{:S(2)}, u32[]{:S(2)}) collective-permute-start(bf16[32,8192]{1,0:T(8,128)(2,1)} %get-tuple-element.39), channel_id=1, source_target_pairs={{0,768},{64,832},{128,896},{192,960},{256,0},{320,64},{384,128},{4... | collective-permute-start | bytes 1572872 | tf_op jit(solution)/shard_map/ppermute | solution.py:66
  70.3 3.0 %collective-permute-start.8 = (bf16[32,8192]{1,0:T(8,128)(2,1)}, bf16[32,8192]{1,0:T(8,128)(2,1)}, u32[]{:S(2)}, u32[]{:S(2)}) collective-permute-start(bf16[32,8192]{1,0:T(8,128)(2,1)} %get-tuple-element.40), channel_id=1, source_target_pairs={{0,512},{64,576},{128,640},{192,704},{256,768},{320,832},{384,896}... | collective-permute-start | bytes 1572872 | tf_op jit(solution)/shard_map/ppermute | solution.py:66
  75.4 3.6 %reshape.293 = f32[16,128,257]{2,1,0:T(8,128)} reshape(f32[16,32896]{1,0:T(8,128)S(1)} %pad.4) | data formatting | bytes 4210688 | tf_op jit(solution)/shard_map/reshape | solution.py:100
  81.2 12.4 %collective-permute-start.10 = (f32[16,128]{1,0:T(8,128)S(1)}, f32[16,128]{1,0:T(8,128)S(1)}, u32[]{:S(2)}, u32[]{:S(2)}) collective-permute-start(f32[16,128]{1,0:T(8,128)S(1)} %slice.68), channel_id=1, source_target_pairs={{0,1},{1,0},{2,3},{3,2},{4,5},{5,4},{6,7},{7,6},{8,9},{9,8},{10,11... | collective-permute-start | bytes 24584 | tf_op jit(solution)/shard_map/ppermute | solution.py:29
  94.4 6.9 %collective-permute-start.11 = (f32[16,128]{1,0:T(8,128)S(1)}, f32[16,128]{1,0:T(8,128)S(1)}, u32[]{:S(2)}, u32[]{:S(2)}) collective-permute-start(f32[16,128]{1,0:T(8,128)S(1)} %slice_add_fusion), channel_id=1, source_target_pairs={{0,2},{2,0},{4,6},{6,4},{8,10},{10,8},{12,14},{14,12},{16,18},{18,... | collective-permute-start | bytes 24584 | tf_op jit(solution)/shard_map/ppermute | solution.py:29
  105.6 4.7 %collective-permute-start.12 = (f32[8,8192]{1,0:T(8,128)S(1)}, f32[8,8192]{1,0:T(8,128)S(1)}, u32[]{:S(2)}, u32[]{:S(2)}) collective-permute-start(f32[8,8192]{1,0:T(8,128)S(1)} %get-tuple-element.41), channel_id=1, source_target_pairs={{0,64},{64,128},{128,192},{192,0},{256,320},{320,384},{384,448},{4... | collective-permute-start | bytes 786440 | tf_op jit(solution)/shard_map/ppermute | solution.py:66
  110.4 2.4 %collective-permute-start.14 = (f32[8,8192]{1,0:T(8,128)S(1)}, f32[8,8192]{1,0:T(8,128)}, u32[]{:S(2)}, u32[]{:S(2)}) collective-permute-start(f32[8,8192]{1,0:T(8,128)S(1)} %get-tuple-element.42), channel_id=1, source_target_pairs={{0,192},{64,0},{128,64},{192,128},{256,448},{320,256},{384,320},{4... | collective-permute-start | bytes 786440 | tf_op jit(solution)/shard_map/ppermute | solution.py:66
  112.7 2.8 %collective-permute-start.13 = (f32[8,8192]{1,0:T(8,128)S(1)}, f32[8,8192]{1,0:T(8,128)}, u32[]{:S(2)}, u32[]{:S(2)}) collective-permute-start(f32[8,8192]{1,0:T(8,128)S(1)} %get-tuple-element.43), channel_id=1, source_target_pairs={{0,128},{64,192},{128,0},{192,64},{256,384},{320,448},{384,256},{4... | collective-permute-start | bytes 786440 | tf_op jit(solution)/shard_map/ppermute | solution.py:66
  115.5 4.0 %collective-permute-start.15 = (f32[16,128]{1,0:T(8,128)S(1)}, f32[16,128]{1,0:T(8,128)S(1)}, u32[]{:S(2)}, u32[]{:S(2)}) collective-permute-start(f32[16,128]{1,0:T(8,128)S(1)} %add.171), channel_id=1, source_target_pairs={{0,4},{2,6},{4,0},{6,2},{8,12},{10,14},{12,8},{14,10},{16,20},{18,... | collective-permute-start | bytes 24584 | tf_op jit(solution)/shard_map/ppermute | solution.py:29
  121.0 6.4 %collective-permute-start.16 = (f32[16,128]{1,0:T(8,128)S(1)}, f32[16,128]{1,0:T(8,128)}, u32[]{:S(2)}, u32[]{:S(2)}) collective-permute-start(f32[16,128]{1,0:T(8,128)S(1)} %add.181), channel_id=1, source_target_pairs={{0,8},{2,10},{4,12},{6,14},{8,0},{10,2},{12,4},{14,6},{16,24},{18,... | collective-permute-start | bytes 24584 | tf_op jit(solution)/shard_map/ppermute | solution.py:29
  129.2 5.4 %collective-permute-done.13 = f32[8,8192]{1,0:T(8,128)} collective-permute-done((f32[8,8192]{1,0:T(8,128)S(1)}, f32[8,8192]{1,0:T(8,128)}, u32[]{:S(2)}, u32[]{:S(2)}) %collective-permute-start.13) | collective-permute-done | bytes 262176 | tf_op jit(solution)/shard_map/ppermute | solution.py:66
  136.3 12.0 %collective-permute-start.18 = (f32[16,128]{1,0:T(8,128)S(1)}, f32[16,128]{1,0:T(8,128)S(1)}, u32[]{:S(2)}, u32[]{:S(2)}) collective-permute-start(f32[16,128]{1,0:T(8,128)S(1)} %add.182), channel_id=1, source_target_pairs={{0,16},{2,18},{4,20},{6,22},{8,24},{10,26},{12,28},{14,30},{16,0},... | collective-permute-start | bytes 24584 | tf_op jit(solution)/shard_map/ppermute | solution.py:29
  149.3 15.7 %collective-permute-start.19 = (f32[16,128]{1,0:T(8,128)S(1)}, f32[16,128]{1,0:T(8,128)S(1)}, u32[]{:S(2)}, u32[]{:S(2)}) collective-permute-start(f32[16,128]{1,0:T(8,128)S(1)} %add.183), channel_id=1, source_target_pairs={{0,32},{2,34},{4,36},{6,38},{8,40},{10,42},{12,44},{14,46},{16,48}... | collective-permute-start | bytes 24584 | tf_op jit(solution)/shard_map/ppermute | solution.py:29
  (83 shorter events, 34.2 us)
Async XLA Ops:
  0.6 21.9 %collective-permute-start.3 = (bf16[8,8192]{1,0:T(8,128)(2,1)}, bf16[8,8192]{1,0:T(8,128)(2,1)S(1)}, u32[]{:S(2)}, u32[]{:S(2)}) collective-permute-start(bf16[8,8192]{1,0:T(8,128)(2,1)} %bitcast.118), channel_id=1, source_target_pairs={{0,192},{64,0},{128,64},{192,128},{256,448},{320,256},{384,320},{4... | collective-permute-start | bytes 393224 | tf_op jit(solution)/shard_map/ppermute | solution.py:45
  6.7 15.8 %collective-permute-start.2 = (bf16[8,8192]{1,0:T(8,128)(2,1)}, bf16[8,8192]{1,0:T(8,128)(2,1)S(1)}, u32[]{:S(2)}, u32[]{:S(2)}) collective-permute-start(bf16[8,8192]{1,0:T(8,128)(2,1)} %bitcast.119), channel_id=1, source_target_pairs={{0,128},{64,192},{128,0},{192,64},{256,384},{320,448},{384,256},{4... | collective-permute-start | bytes 393224 | tf_op jit(solution)/shard_map/ppermute | solution.py:45
  8.6 13.9 %collective-permute-start.1 = (bf16[8,8192]{1,0:T(8,128)(2,1)}, bf16[8,8192]{1,0:T(8,128)(2,1)S(1)}, u32[]{:S(2)}, u32[]{:S(2)}) collective-permute-start(bf16[8,8192]{1,0:T(8,128)(2,1)} %bitcast.120), channel_id=1, source_target_pairs={{0,64},{64,128},{128,192},{192,0},{256,320},{320,384},{384,448},{4... | collective-permute-start | bytes 393224 | tf_op jit(solution)/shard_map/ppermute | solution.py:45
  12.9 9.0 %collective-permute-start = (bf16[1,127,256]{1,2,0:T(8,128)(2,1)S(1)}, bf16[1,127,256]{1,2,0:T(8,128)(2,1)S(1)}, u32[]{:S(2)}, u32[]{:S(2)}) collective-permute-start(bf16[1,127,256]{1,2,0:T(8,128)(2,1)S(1)} %bitcast.105), channel_id=1, source_target_pairs={{2,0},{4,2},{6,4},{8,6},{10,8},{12,10},{14,12},{16,14},{18,16},{20... | collective-permute-start | bytes 195080 | tf_op jit(solution)/shard_map/ppermute | solution.py:12
  17.8 4.7 %copy-start.1 = (bf16[1,1,8,8192]{3,2,1,0:T(8,128)(2,1)S(1)}, bf16[1,1,8,8192]{3,2,1,0:T(8,128)(2,1)}, u32[]{:S(2)}) copy-start(bf16[1,1,8,8192]{3,2,1,0:T(8,128)(2,1)} %param.9) | copy-start | bytes 393220
  23.3 17.0 %collective-permute-start.6 = (bf16[4,8,8192]{2,1,0:T(8,128)(2,1)S(1)}, bf16[4,8,8192]{2,1,0:T(8,128)(2,1)S(1)}, u32[]{:S(2)}, u32[]{:S(2)}) collective-permute-start(bf16[4,8,8192]{2,1,0:T(8,128)(2,1)S(1)} %broadcast_select_fusion), channel_id=1, source_target_pairs={{0,768},{64,832},{128,896},{192,960},{256,0},{320,64},{384,128},{4... | collective-permute-start | bytes 1572872 | tf_op jit(solution)/shard_map/ppermute | solution.py:50
  27.7 12.6 %collective-permute-start.5 = (bf16[4,8,8192]{2,1,0:T(8,128)(2,1)S(1)}, bf16[4,8,8192]{2,1,0:T(8,128)(2,1)S(1)}, u32[]{:S(2)}, u32[]{:S(2)}) collective-permute-start(bf16[4,8,8192]{2,1,0:T(8,128)(2,1)S(1)} %broadcast_select_fusion), channel_id=1, source_target_pairs={{0,512},{64,576},{128,640},{192,704},{256,768},{320,832},{384,896}... | collective-permute-start | bytes 1572872 | tf_op jit(solution)/shard_map/ppermute | solution.py:50
  30.2 15.5 %collective-permute-start.4 = (bf16[4,8,8192]{2,1,0:T(8,128)(2,1)S(1)}, bf16[4,8,8192]{2,1,0:T(8,128)(2,1)S(1)}, u32[]{:S(2)}, u32[]{:S(2)}) collective-permute-start(bf16[4,8,8192]{2,1,0:T(8,128)(2,1)S(1)} %broadcast_select_fusion), channel_id=1, source_target_pairs={{0,256},{64,320},{128,384},{192,448},{256,512},{320,576},{384,640}... | collective-permute-start | bytes 1572872 | tf_op jit(solution)/shard_map/ppermute | solution.py:50
  61.2 1.4 copy-start
  63.8 39.9 %collective-permute-start.7 = (bf16[32,8192]{1,0:T(8,128)(2,1)}, bf16[32,8192]{1,0:T(8,128)(2,1)}, u32[]{:S(2)}, u32[]{:S(2)}) collective-permute-start(bf16[32,8192]{1,0:T(8,128)(2,1)} %get-tuple-element.38), channel_id=1, source_target_pairs={{0,256},{64,320},{128,384},{192,448},{256,512},{320,576},{384,640}... | collective-permute-start | bytes 1572872 | tf_op jit(solution)/shard_map/ppermute | solution.py:66
  67.7 36.0 %collective-permute-start.9 = (bf16[32,8192]{1,0:T(8,128)(2,1)}, bf16[32,8192]{1,0:T(8,128)(2,1)}, u32[]{:S(2)}, u32[]{:S(2)}) collective-permute-start(bf16[32,8192]{1,0:T(8,128)(2,1)} %get-tuple-element.39), channel_id=1, source_target_pairs={{0,768},{64,832},{128,896},{192,960},{256,0},{320,64},{384,128},{4... | collective-permute-start | bytes 1572872 | tf_op jit(solution)/shard_map/ppermute | solution.py:66
  70.3 33.4 %collective-permute-start.8 = (bf16[32,8192]{1,0:T(8,128)(2,1)}, bf16[32,8192]{1,0:T(8,128)(2,1)}, u32[]{:S(2)}, u32[]{:S(2)}) collective-permute-start(bf16[32,8192]{1,0:T(8,128)(2,1)} %get-tuple-element.40), channel_id=1, source_target_pairs={{0,512},{64,576},{128,640},{192,704},{256,768},{320,832},{384,896}... | collective-permute-start | bytes 1572872 | tf_op jit(solution)/shard_map/ppermute | solution.py:66
  81.2 13.2 %collective-permute-start.10 = (f32[16,128]{1,0:T(8,128)S(1)}, f32[16,128]{1,0:T(8,128)S(1)}, u32[]{:S(2)}, u32[]{:S(2)}) collective-permute-start(f32[16,128]{1,0:T(8,128)S(1)} %slice.68), channel_id=1, source_target_pairs={{0,1},{1,0},{2,3},{3,2},{4,5},{5,4},{6,7},{7,6},{8,9},{9,8},{10,11... | collective-permute-start | bytes 24584 | tf_op jit(solution)/shard_map/ppermute | solution.py:29
  94.4 9.3 %collective-permute-start.11 = (f32[16,128]{1,0:T(8,128)S(1)}, f32[16,128]{1,0:T(8,128)S(1)}, u32[]{:S(2)}, u32[]{:S(2)}) collective-permute-start(f32[16,128]{1,0:T(8,128)S(1)} %slice_add_fusion), channel_id=1, source_target_pairs={{0,2},{2,0},{4,6},{6,4},{8,10},{10,8},{12,14},{14,12},{16,18},{18,... | collective-permute-start | bytes 24584 | tf_op jit(solution)/shard_map/ppermute | solution.py:29
  101.4 25.9 %collective-permute-start.17 = (bf16[1,127,256]{2,1,0:T(8,128)(2,1)S(1)}, bf16[1,127,256]{2,1,0:T(8,128)(2,1)S(1)}, u32[]{:S(2)}, u32[]{:S(2)}) collective-permute-start(bf16[1,127,256]{2,1,0:T(8,128)(2,1)S(1)} %slice.69), channel_id=1, source_target_pairs={{0,2},{2,4},{4,6},{6,8},{8,10},{10,12},{12,14},{14,16},{16,18},{18... | collective-permute-start | bytes 195080 | tf_op jit(solution)/shard_map/ppermute | solution.py:12
  105.6 23.5 %collective-permute-start.12 = (f32[8,8192]{1,0:T(8,128)S(1)}, f32[8,8192]{1,0:T(8,128)S(1)}, u32[]{:S(2)}, u32[]{:S(2)}) collective-permute-start(f32[8,8192]{1,0:T(8,128)S(1)} %get-tuple-element.41), channel_id=1, source_target_pairs={{0,64},{64,128},{128,192},{192,0},{256,320},{320,384},{384,448},{4... | collective-permute-start | bytes 786440 | tf_op jit(solution)/shard_map/ppermute | solution.py:66
  110.4 18.8 %collective-permute-start.14 = (f32[8,8192]{1,0:T(8,128)S(1)}, f32[8,8192]{1,0:T(8,128)}, u32[]{:S(2)}, u32[]{:S(2)}) collective-permute-start(f32[8,8192]{1,0:T(8,128)S(1)} %get-tuple-element.42), channel_id=1, source_target_pairs={{0,192},{64,0},{128,64},{192,128},{256,448},{320,256},{384,320},{4... | collective-permute-start | bytes 786440 | tf_op jit(solution)/shard_map/ppermute | solution.py:66
  112.7 21.8 %collective-permute-start.13 = (f32[8,8192]{1,0:T(8,128)S(1)}, f32[8,8192]{1,0:T(8,128)}, u32[]{:S(2)}, u32[]{:S(2)}) collective-permute-start(f32[8,8192]{1,0:T(8,128)S(1)} %get-tuple-element.43), channel_id=1, source_target_pairs={{0,128},{64,192},{128,0},{192,64},{256,384},{320,448},{384,256},{4... | collective-permute-start | bytes 786440 | tf_op jit(solution)/shard_map/ppermute | solution.py:66
  115.5 5.4 %collective-permute-start.15 = (f32[16,128]{1,0:T(8,128)S(1)}, f32[16,128]{1,0:T(8,128)S(1)}, u32[]{:S(2)}, u32[]{:S(2)}) collective-permute-start(f32[16,128]{1,0:T(8,128)S(1)} %add.171), channel_id=1, source_target_pairs={{0,4},{2,6},{4,0},{6,2},{8,12},{10,14},{12,8},{14,10},{16,20},{18,... | collective-permute-start | bytes 24584 | tf_op jit(solution)/shard_map/ppermute | solution.py:29
  121.0 7.5 %collective-permute-start.16 = (f32[16,128]{1,0:T(8,128)S(1)}, f32[16,128]{1,0:T(8,128)}, u32[]{:S(2)}, u32[]{:S(2)}) collective-permute-start(f32[16,128]{1,0:T(8,128)S(1)} %add.181), channel_id=1, source_target_pairs={{0,8},{2,10},{4,12},{6,14},{8,0},{10,2},{12,4},{14,6},{16,24},{18,... | collective-permute-start | bytes 24584 | tf_op jit(solution)/shard_map/ppermute | solution.py:29
  136.3 13.0 %collective-permute-start.18 = (f32[16,128]{1,0:T(8,128)S(1)}, f32[16,128]{1,0:T(8,128)S(1)}, u32[]{:S(2)}, u32[]{:S(2)}) collective-permute-start(f32[16,128]{1,0:T(8,128)S(1)} %add.182), channel_id=1, source_target_pairs={{0,16},{2,18},{4,20},{6,22},{8,24},{10,26},{12,28},{14,30},{16,0},... | collective-permute-start | bytes 24584 | tf_op jit(solution)/shard_map/ppermute | solution.py:29
  149.3 16.7 %collective-permute-start.19 = (f32[16,128]{1,0:T(8,128)S(1)}, f32[16,128]{1,0:T(8,128)S(1)}, u32[]{:S(2)}, u32[]{:S(2)}) collective-permute-start(f32[16,128]{1,0:T(8,128)S(1)} %add.183), channel_id=1, source_target_pairs={{0,32},{2,34},{4,36},{6,38},{8,40},{10,42},{12,44},{14,46},{16,48}... | collective-permute-start | bytes 24584 | tf_op jit(solution)/shard_map/ppermute | solution.py:29

commit v5 on v4

--- a/solution.py
+++ b/solution.py
@@ -148,15 +148,18 @@
     grad_in = jnp.concatenate([grad_conv * value_in, grad_conv * second_in], axis=-1).astype(
         jnp.bfloat16
     )
-    partials = jnp.einsum(
-        "bnjc,djc->bnd",
-        grad_in.reshape(grad_in.shape[:2] + (2, channels)),
-        w_in,
-        preferred_element_type=jnp.float32,
-    )
+
+    def row_chunks(grad_in):
+        partials = jnp.einsum(
+            "bnjc,djc->bnd",
+            grad_in.reshape(grad_in.shape[:2] + (2, channels)),
+            w_in,
+            preferred_element_type=jnp.float32,
+        )
+        partial_rows = partials[0].astype(jnp.bfloat16)
+        return partial_rows.reshape((outer, -1) + partial_rows.shape[1:])
+
     outer = lax.axis_size("tensor") // inner
-    partial_rows = partials[0].astype(jnp.bfloat16)
-    x_chunks = partial_rows.reshape((outer, -1) + partial_rows.shape[1:])
     grad_ahead = jnp.concatenate(
         [grad_mix, next_rows_in, jnp.zeros((seq_count, 1, channels), jnp.bfloat16)], axis=1
     ).reshape(seq_count, stretch_rows + tap_count, groups, group_size)
@@ -169,13 +172,17 @@
     local_grad = band_sums_ahead(products, tap_count)
     if lax.axis_size("context") & (lax.axis_size("context") - 1) or lax.axis_size("dp") & (lax.axis_size("dp") - 1):
         summed = lax.psum(local_grad, ("context", "dp"))
+        x_chunks = row_chunks(grad_in)
         x_sums = scatter_stage(x_chunks, "tensor", inner, True, False)
         d_tokens = scatter_stage(x_sums.reshape((inner, -1) + x_sums.shape[1:]), "tensor", inner, False, True)
     else:
         context_steps = [1 << k for k in range(lax.axis_size("context").bit_length() - 1)]
         dp_steps = [1 << k for k in range(lax.axis_size("dp").bit_length() - 1)]
         first, second, third = context_steps[:1], context_steps[1:3], context_steps[3:]
-        summed = butterfly_rounds(butterfly_rounds(local_grad, "dp", dp_steps), "context", first)
+        summed = butterfly_rounds(local_grad, "dp", dp_steps)
+        grad_in, summed = lax.optimization_barrier((grad_in, summed))
+        summed = butterfly_rounds(summed, "context", first)
+        x_chunks = row_chunks(grad_in)
         x_sums = scatter_stage(x_chunks, "tensor", inner, True, False)
         x_sums, summed = lax.optimization_barrier((x_sums, summed))
         summed = butterfly_rounds(summed, "context", second)

time: 169 us -> 177 us (1.047)
  the two profiles are of different devices: /device:TPU:1 before, /device:TPU:6 now
where the time goes in v5:
time: 177 us; the launch traced here: 176 us
  starting transfers between devices  100 us (56%)
  waiting for transfers between devices  35.8 us (20%)
  local copies, waits for them, and re-layouts  15.9 us (9%)
  matrix products  12.4 us (7%)
  other arithmetic  10.7 us (6%)
    ppermute x6, starting transfers between devices, butterfly_rounds(): lax.ppermute(value, axis, [(i, i ^ step) for i in range(count)])  47.2 us
    ppermute x6, starting transfers between devices, scatter_stage(): lax.ppermute(sent, axis, grid_shift(axis, s, inner, outer_step))  20.6 us
    ppermute x3, starting transfers between devices, grid_gather(): lax.ppermute(stage, axis, grid_shift(axis, s, inner, True))  17.6 us
    ppermute x6, waiting for transfers between devices, scatter_stage(): lax.ppermute(sent, axis, grid_shift(axis, s, inner, outer_step))  14.7 us
    ppermute x3, waiting for transfers between devices, grid_gather(): lax.ppermute(stage, axis, grid_shift(axis, s, inner, True))  10.8 us
    ppermute x3, starting transfers between devices, grid_gather(): lax.ppermute(rows, axis, grid_shift(axis, s, inner, False))  10.3 us
    dot_general x1, matrix products, row_chunks(): jnp.einsum('bnjc,djc->bnd', grad_in.reshape(grad_in.shape[:2] + (2, chann...  6.22 us
    ppermute x6, waiting for transfers between devices, butterfly_rounds(): lax.ppermute(value, axis, [(i, i ^ step) for i in range(count)])  5.43 us
  transfers between devices with their start and end apart: 20, of which 12 were waited for; matrix products, arithmetic and copies ran while one was open for 6% of the time, Pallas kernels for 0%

profile of v5, /device:TPU:6, one launch (start us, length us, event | category | flops | bytes accessed | tf_op | source)
XLA Modules:
  0.0 176.4 jit_solution(1000770225359067792)
XLA Ops:
  0.6 5.5 %collective-permute-start.3 = (bf16[8,8192]{1,0:T(8,128)(2,1)}, bf16[8,8192]{1,0:T(8,128)(2,1)S(1)}, u32[]{:S(2)}, u32[]{:S(2)}) collective-permute-start(bf16[8,8192]{1,0:T(8,128)(2,1)} %bitcast.120), channel_id=1, source_target_pairs={{0,192},{64,0},{128,64},{192,128},{256,448},{320,256},{384,320},{4... | collective-permute-start | bytes 393224 | tf_op jit(solution)/shard_map/ppermute | solution.py:45
  8.1 2.9 %collective-permute-start.1 = (bf16[8,8192]{1,0:T(8,128)(2,1)}, bf16[8,8192]{1,0:T(8,128)(2,1)S(1)}, u32[]{:S(2)}, u32[]{:S(2)}) collective-permute-start(bf16[8,8192]{1,0:T(8,128)(2,1)} %bitcast.122), channel_id=1, source_target_pairs={{0,64},{64,128},{128,192},{192,0},{256,320},{320,384},{384,448},{4... | collective-permute-start | bytes 393224 | tf_op jit(solution)/shard_map/ppermute | solution.py:45
  18.2 4.9 %collective-permute-done = bf16[1,127,256]{1,2,0:T(8,128)(2,1)S(1)} collective-permute-done((bf16[1,127,256]{1,2,0:T(8,128)(2,1)S(1)}, bf16[1,127,256]{1,2,0:T(8,128)(2,1)S(1)}, u32[]{:S(2)}, u32[]{:S(2)}) %collective-permute-start) | collective-permute-done | bytes 65056 | tf_op jit(solution)/shard_map/ppermute | solution.py:12
  24.4 2.7 %collective-permute-start.6 = (bf16[4,8,8192]{2,1,0:T(8,128)(2,1)S(1)}, bf16[4,8,8192]{2,1,0:T(8,128)(2,1)S(1)}, u32[]{:S(2)}, u32[]{:S(2)}) collective-permute-start(bf16[4,8,8192]{2,1,0:T(8,128)(2,1)S(1)} %broadcast_select_fusion), channel_id=1, source_target_pairs={{0,768},{64,832},{128,896},{192,960},{256,0},{320,64},{384,128},{4... | collective-permute-start | bytes 1572872 | tf_op jit(solution)/shard_map/ppermute | solution.py:50
  27.1 13.0 %collective-permute-start.5 = (bf16[4,8,8192]{2,1,0:T(8,128)(2,1)S(1)}, bf16[4,8,8192]{2,1,0:T(8,128)(2,1)S(1)}, u32[]{:S(2)}, u32[]{:S(2)}) collective-permute-start(bf16[4,8,8192]{2,1,0:T(8,128)(2,1)S(1)} %broadcast_select_fusion), channel_id=1, source_target_pairs={{0,512},{64,576},{128,640},{192,704},{256,768},{320,832},{384,896}... | collective-permute-start | bytes 1572872 | tf_op jit(solution)/shard_map/ppermute | solution.py:50
  42.2 2.6 %collective-permute-done.6 = bf16[4,8,8192]{2,1,0:T(8,128)(2,1)S(1)} collective-permute-done((bf16[4,8,8192]{2,1,0:T(8,128)(2,1)S(1)}, bf16[4,8,8192]{2,1,0:T(8,128)(2,1)S(1)}, u32[]{:S(2)}, u32[]{:S(2)}) %collective-permute-start.6) | collective-permute-done | bytes 524320 | tf_op jit(solution)/shard_map/ppermute | solution.py:50
  44.8 6.2 %collective-permute-done.5 = bf16[4,8,8192]{2,1,0:T(8,128)(2,1)S(1)} collective-permute-done((bf16[4,8,8192]{2,1,0:T(8,128)(2,1)S(1)}, bf16[4,8,8192]{2,1,0:T(8,128)(2,1)S(1)}, u32[]{:S(2)}, u32[]{:S(2)}) %collective-permute-start.5) | collective-permute-done | bytes 524320 | tf_op jit(solution)/shard_map/ppermute | solution.py:50
  57.1 4.7 %fusion.5 = bf16[128,2,256]{2,0,1:T(8,128)(2,1)S(1)} fusion(bf16[8192,2,256]{2,1,0:T(2,128)(2,1)} %param.10, bf16[128,8192]{1,0:T(8,128)(2,1)S(1)} %bitcast_select_fusion), kind=kOutput, calls=%fused_computation.11 | convolution fusion | flops 1073807360 | bytes 10616832 | tf_op jit(solution)/shard_map/nd,djc->njc/dot_general | solution.py:114
  64.5 3.6 %reshape.307 = f32[16,128,257]{2,1,0:T(8,128)} reshape(f32[16,32896]{1,0:T(8,128)S(1)} %pad.4) | data formatting | bytes 4210688 | tf_op jit(solution)/shard_map/reshape | solution.py:100
  73.5 6.2 %fusion = bf16[4,32,8192]{2,1,0:T(8,128)(2,1)S(1)} fusion(bf16[4,32,256,2]{2,1,0,3:T(8,128)(2,1)S(1)} %bitcast.119, bf16[8192,2,256,1]{2,1,0,3:T(2,128)(2,1)} %bitcast.128), kind=kOutput, calls=%fused_computation.3 | convolution fusion | flops 1074790400 | bytes 10616832 | tf_op jit(solution)/shard_map/bnjc,djc->bnd/dot_general | solution.py:153
  81.2 4.5 %collective-permute-start.8 = (bf16[32,8192]{1,0:T(8,128)(2,1)S(1)}, bf16[32,8192]{1,0:T(8,128)(2,1)S(1)}, u32[]{:S(2)}, u32[]{:S(2)}) collective-permute-start(bf16[32,8192]{1,0:T(8,128)(2,1)S(1)} %get-tuple-element.42), channel_id=1, source_target_pairs={{0,256},{64,320},{128,384},{192,448},{256,512},{320,576},{384,640}... | collective-permute-start | bytes 1572872 | tf_op jit(solution)/shard_map/ppermute | solution.py:66
  87.7 3.4 %collective-permute-start.9 = (bf16[32,8192]{1,0:T(8,128)(2,1)S(1)}, bf16[32,8192]{1,0:T(8,128)(2,1)}, u32[]{:S(2)}, u32[]{:S(2)}) collective-permute-start(bf16[32,8192]{1,0:T(8,128)(2,1)S(1)} %get-tuple-element.44), channel_id=1, source_target_pairs={{0,512},{64,576},{128,640},{192,704},{256,768},{320,832},{384,896}... | collective-permute-start | bytes 1572872 | tf_op jit(solution)/shard_map/ppermute | solution.py:66
  91.1 7.2 %collective-permute-start.11 = (f32[16,128]{1,0:T(8,128)S(1)}, f32[16,128]{1,0:T(8,128)S(1)}, u32[]{:S(2)}, u32[]{:S(2)}) collective-permute-start(f32[16,128]{1,0:T(8,128)S(1)} %slice_add_fusion), channel_id=1, source_target_pairs={{0,2},{2,0},{4,6},{6,4},{8,10},{10,8},{12,14},{14,12},{16,18},{18,... | collective-permute-start | bytes 24584 | tf_op jit(solution)/shard_map/ppermute | solution.py:29
  99.0 3.2 %collective-permute-start.17 = (bf16[1,127,256]{1,2,0:T(8,128)(2,1)}, bf16[1,127,256]{1,2,0:T(8,128)(2,1)}, u32[]{:S(2)}, u32[]{:S(2)}) collective-permute-start(bf16[1,127,256]{1,2,0:T(8,128)(2,1)} %slice.69), channel_id=1, source_target_pairs={{0,2},{2,4},{4,6},{6,8},{8,10},{10,12},{12,14},{14,16},{16,18},{18... | collective-permute-start | bytes 195080 | tf_op jit(solution)/shard_map/ppermute | solution.py:12
  102.2 6.3 %collective-permute-done.8 = bf16[32,8192]{1,0:T(8,128)(2,1)S(1)} collective-permute-done((bf16[32,8192]{1,0:T(8,128)(2,1)S(1)}, bf16[32,8192]{1,0:T(8,128)(2,1)S(1)}, u32[]{:S(2)}, u32[]{:S(2)}) %collective-permute-start.8) | collective-permute-done | bytes 524320 | tf_op jit(solution)/shard_map/ppermute | solution.py:66
  108.5 5.4 %collective-permute-done.10 = bf16[32,8192]{1,0:T(8,128)(2,1)} collective-permute-done((bf16[32,8192]{1,0:T(8,128)(2,1)S(1)}, bf16[32,8192]{1,0:T(8,128)(2,1)}, u32[]{:S(2)}, u32[]{:S(2)}) %collective-permute-start.10) | collective-permute-done | bytes 524320 | tf_op jit(solution)/shard_map/ppermute | solution.py:66
  115.6 5.0 %collective-permute-start.12 = (f32[8,8192]{1,0:T(8,128)S(1)}, f32[8,8192]{1,0:T(8,128)S(1)}, u32[]{:S(2)}, u32[]{:S(2)}) collective-permute-start(f32[8,8192]{1,0:T(8,128)S(1)} %get-tuple-element.45), channel_id=1, source_target_pairs={{0,64},{64,128},{128,192},{192,0},{256,320},{320,384},{384,448},{4... | collective-permute-start | bytes 786440 | tf_op jit(solution)/shard_map/ppermute | solution.py:66
  120.6 2.6 %collective-permute-start.14 = (f32[8,8192]{1,0:T(8,128)S(1)}, f32[8,8192]{1,0:T(8,128)}, u32[]{:S(2)}, u32[]{:S(2)}) collective-permute-start(f32[8,8192]{1,0:T(8,128)S(1)} %get-tuple-element.46), channel_id=1, source_target_pairs={{0,192},{64,0},{128,64},{192,128},{256,448},{320,256},{384,320},{4... | collective-permute-start | bytes 786440 | tf_op jit(solution)/shard_map/ppermute | solution.py:66
  123.3 3.1 %collective-permute-start.13 = (f32[8,8192]{1,0:T(8,128)S(1)}, f32[8,8192]{1,0:T(8,128)}, u32[]{:S(2)}, u32[]{:S(2)}) collective-permute-start(f32[8,8192]{1,0:T(8,128)S(1)} %get-tuple-element.47), channel_id=1, source_target_pairs={{0,128},{64,192},{128,0},{192,64},{256,384},{320,448},{384,256},{4... | collective-permute-start | bytes 786440 | tf_op jit(solution)/shard_map/ppermute | solution.py:66
  126.4 4.2 %collective-permute-start.15 = (f32[16,128]{1,0:T(8,128)S(1)}, f32[16,128]{1,0:T(8,128)S(1)}, u32[]{:S(2)}, u32[]{:S(2)}) collective-permute-start(f32[16,128]{1,0:T(8,128)S(1)} %add.171), channel_id=1, source_target_pairs={{0,4},{2,6},{4,0},{6,2},{8,12},{10,14},{12,8},{14,10},{16,20},{18,... | collective-permute-start | bytes 24584 | tf_op jit(solution)/shard_map/ppermute | solution.py:29
  132.2 6.6 %collective-permute-start.16 = (f32[16,128]{1,0:T(8,128)S(1)}, f32[16,128]{1,0:T(8,128)S(1)}, u32[]{:S(2)}, u32[]{:S(2)}) collective-permute-start(f32[16,128]{1,0:T(8,128)S(1)} %add.181), channel_id=1, source_target_pairs={{0,8},{2,10},{4,12},{6,14},{8,0},{10,2},{12,4},{14,6},{16,24},{18,... | collective-permute-start | bytes 24584 | tf_op jit(solution)/shard_map/ppermute | solution.py:29
  140.5 3.0 %collective-permute-done.13 = f32[8,8192]{1,0:T(8,128)} collective-permute-done((f32[8,8192]{1,0:T(8,128)S(1)}, f32[8,8192]{1,0:T(8,128)}, u32[]{:S(2)}, u32[]{:S(2)}) %collective-permute-start.13) | collective-permute-done | bytes 262176 | tf_op jit(solution)/shard_map/ppermute | solution.py:66
  145.2 10.9 %collective-permute-start.18 = (f32[16,128]{1,0:T(8,128)S(1)}, f32[16,128]{1,0:T(8,128)S(1)}, u32[]{:S(2)}, u32[]{:S(2)}) collective-permute-start(f32[16,128]{1,0:T(8,128)S(1)} %add.182), channel_id=1, source_target_pairs={{0,16},{2,18},{4,20},{6,22},{8,24},{10,26},{12,28},{14,30},{16,0},... | collective-permute-start | bytes 24584 | tf_op jit(solution)/shard_map/ppermute | solution.py:29
  157.7 16.4 %collective-permute-start.19 = (f32[16,128]{1,0:T(8,128)S(1)}, f32[16,128]{1,0:T(8,128)S(1)}, u32[]{:S(2)}, u32[]{:S(2)}) collective-permute-start(f32[16,128]{1,0:T(8,128)S(1)} %add.183), channel_id=1, source_target_pairs={{0,32},{2,34},{4,36},{6,38},{8,40},{10,42},{12,44},{14,46},{16,48}... | collective-permute-start | bytes 24584 | tf_op jit(solution)/shard_map/ppermute | solution.py:29
  (85 shorter events, 40.9 us)
Async XLA Ops:
  0.6 22.9 %collective-permute-start.3 = (bf16[8,8192]{1,0:T(8,128)(2,1)}, bf16[8,8192]{1,0:T(8,128)(2,1)S(1)}, u32[]{:S(2)}, u32[]{:S(2)}) collective-permute-start(bf16[8,8192]{1,0:T(8,128)(2,1)} %bitcast.120), channel_id=1, source_target_pairs={{0,192},{64,0},{128,64},{192,128},{256,448},{320,256},{384,320},{4... | collective-permute-start | bytes 393224 | tf_op jit(solution)/shard_map/ppermute | solution.py:45
  6.1 17.4 %collective-permute-start.2 = (bf16[8,8192]{1,0:T(8,128)(2,1)}, bf16[8,8192]{1,0:T(8,128)(2,1)S(1)}, u32[]{:S(2)}, u32[]{:S(2)}) collective-permute-start(bf16[8,8192]{1,0:T(8,128)(2,1)} %bitcast.121), channel_id=1, source_target_pairs={{0,128},{64,192},{128,0},{192,64},{256,384},{320,448},{384,256},{4... | collective-permute-start | bytes 393224 | tf_op jit(solution)/shard_map/ppermute | solution.py:45
  8.1 15.5 %collective-permute-start.1 = (bf16[8,8192]{1,0:T(8,128)(2,1)}, bf16[8,8192]{1,0:T(8,128)(2,1)S(1)}, u32[]{:S(2)}, u32[]{:S(2)}) collective-permute-start(bf16[8,8192]{1,0:T(8,128)(2,1)} %bitcast.122), channel_id=1, source_target_pairs={{0,64},{64,128},{128,192},{192,0},{256,320},{320,384},{384,448},{4... | collective-permute-start | bytes 393224 | tf_op jit(solution)/shard_map/ppermute | solution.py:45
  12.9 10.2 %collective-permute-start = (bf16[1,127,256]{1,2,0:T(8,128)(2,1)S(1)}, bf16[1,127,256]{1,2,0:T(8,128)(2,1)S(1)}, u32[]{:S(2)}, u32[]{:S(2)}) collective-permute-start(bf16[1,127,256]{1,2,0:T(8,128)(2,1)S(1)} %bitcast.107), channel_id=1, source_target_pairs={{2,0},{4,2},{6,4},{8,6},{10,8},{12,10},{14,12},{16,14},{18,16},{20... | collective-permute-start | bytes 195080 | tf_op jit(solution)/shard_map/ppermute | solution.py:12
  17.7 5.9 %copy-start.4 = (bf16[1,1,8,8192]{3,2,1,0:T(8,128)(2,1)S(1)}, bf16[1,1,8,8192]{3,2,1,0:T(8,128)(2,1)}, u32[]{:S(2)}) copy-start(bf16[1,1,8,8192]{3,2,1,0:T(8,128)(2,1)} %param.9) | copy-start | bytes 393220
  24.4 20.4 %collective-permute-start.6 = (bf16[4,8,8192]{2,1,0:T(8,128)(2,1)S(1)}, bf16[4,8,8192]{2,1,0:T(8,128)(2,1)S(1)}, u32[]{:S(2)}, u32[]{:S(2)}) collective-permute-start(bf16[4,8,8192]{2,1,0:T(8,128)(2,1)S(1)} %broadcast_select_fusion), channel_id=1, source_target_pairs={{0,768},{64,832},{128,896},{192,960},{256,0},{320,64},{384,128},{4... | collective-permute-start | bytes 1572872 | tf_op jit(solution)/shard_map/ppermute | solution.py:50
  27.1 23.8 %collective-permute-start.5 = (bf16[4,8,8192]{2,1,0:T(8,128)(2,1)S(1)}, bf16[4,8,8192]{2,1,0:T(8,128)(2,1)S(1)}, u32[]{:S(2)}, u32[]{:S(2)}) collective-permute-start(bf16[4,8,8192]{2,1,0:T(8,128)(2,1)S(1)} %broadcast_select_fusion), channel_id=1, source_target_pairs={{0,512},{64,576},{128,640},{192,704},{256,768},{320,832},{384,896}... | collective-permute-start | bytes 1572872 | tf_op jit(solution)/shard_map/ppermute | solution.py:50
  40.1 12.9 %collective-permute-start.4 = (bf16[4,8,8192]{2,1,0:T(8,128)(2,1)S(1)}, bf16[4,8,8192]{2,1,0:T(8,128)(2,1)S(1)}, u32[]{:S(2)}, u32[]{:S(2)}) collective-permute-start(bf16[4,8,8192]{2,1,0:T(8,128)(2,1)S(1)} %broadcast_select_fusion), channel_id=1, source_target_pairs={{0,256},{64,320},{128,384},{192,448},{256,512},{320,576},{384,640}... | collective-permute-start | bytes 1572872 | tf_op jit(solution)/shard_map/ppermute | solution.py:50
  57.1 5.5 %copy-start.3 = (bf16[1,127,256]{1,2,0:T(8,128)(2,1)S(1)}, bf16[1,127,256]{1,2,0:T(8,128)(2,1)}, u32[]{:S(2)}) copy-start(bf16[1,127,256]{1,2,0:T(8,128)(2,1)} %copy-done.2) | copy-start | bytes 195076
  68.2 4.1 %copy-start.1 = (bf16[1,128,256]{1,2,0:T(8,128)(2,1)S(1)}, bf16[1,128,256]{1,2,0:T(8,128)(2,1)}, u32[]{:S(2)}) copy-start(bf16[1,128,256]{1,2,0:T(8,128)(2,1)} %get-tuple-element.49) | copy-start | bytes 196612
  70.3 3.1 %collective-permute-start.7 = (f32[16,128]{1,0:T(8,128)S(1)}, f32[16,128]{1,0:T(8,128)S(1)}, u32[]{:S(2)}, u32[]{:S(2)}) collective-permute-start(f32[16,128]{1,0:T(8,128)S(1)} %slice.68), channel_id=1, source_target_pairs={{0,1},{1,0},{2,3},{3,2},{4,5},{5,4},{6,7},{7,6},{8,9},{9,8},{10,11... | collective-permute-start | bytes 24584 | tf_op jit(solution)/shard_map/ppermute | solution.py:29
  79.7 1.3 copy-start
  81.2 27.3 %collective-permute-start.8 = (bf16[32,8192]{1,0:T(8,128)(2,1)S(1)}, bf16[32,8192]{1,0:T(8,128)(2,1)S(1)}, u32[]{:S(2)}, u32[]{:S(2)}) collective-permute-start(bf16[32,8192]{1,0:T(8,128)(2,1)S(1)} %get-tuple-element.42), channel_id=1, source_target_pairs={{0,256},{64,320},{128,384},{192,448},{256,512},{320,576},{384,640}... | collective-permute-start | bytes 1572872 | tf_op jit(solution)/shard_map/ppermute | solution.py:66
  85.7 28.2 %collective-permute-start.10 = (bf16[32,8192]{1,0:T(8,128)(2,1)S(1)}, bf16[32,8192]{1,0:T(8,128)(2,1)}, u32[]{:S(2)}, u32[]{:S(2)}) collective-permute-start(bf16[32,8192]{1,0:T(8,128)(2,1)S(1)} %get-tuple-element.43), channel_id=1, source_target_pairs={{0,768},{64,832},{128,896},{192,960},{256,0},{320,64},{384,128},{4... | collective-permute-start | bytes 1572872 | tf_op jit(solution)/shard_map/ppermute | solution.py:66
  87.7 26.2 %collective-permute-start.9 = (bf16[32,8192]{1,0:T(8,128)(2,1)S(1)}, bf16[32,8192]{1,0:T(8,128)(2,1)}, u32[]{:S(2)}, u32[]{:S(2)}) collective-permute-start(bf16[32,8192]{1,0:T(8,128)(2,1)S(1)} %get-tuple-element.44), channel_id=1, source_target_pairs={{0,512},{64,576},{128,640},{192,704},{256,768},{320,832},{384,896}... | collective-permute-start | bytes 1572872 | tf_op jit(solution)/shard_map/ppermute | solution.py:66
  91.1 11.2 %collective-permute-start.11 = (f32[16,128]{1,0:T(8,128)S(1)}, f32[16,128]{1,0:T(8,128)S(1)}, u32[]{:S(2)}, u32[]{:S(2)}) collective-permute-start(f32[16,128]{1,0:T(8,128)S(1)} %slice_add_fusion), channel_id=1, source_target_pairs={{0,2},{2,0},{4,6},{6,4},{8,10},{10,8},{12,14},{14,12},{16,18},{18,... | collective-permute-start | bytes 24584 | tf_op jit(solution)/shard_map/ppermute | solution.py:29
  99.0 39.9 %collective-permute-start.17 = (bf16[1,127,256]{1,2,0:T(8,128)(2,1)}, bf16[1,127,256]{1,2,0:T(8,128)(2,1)}, u32[]{:S(2)}, u32[]{:S(2)}) collective-permute-start(bf16[1,127,256]{1,2,0:T(8,128)(2,1)} %slice.69), channel_id=1, source_target_pairs={{0,2},{2,4},{4,6},{6,8},{8,10},{10,12},{12,14},{14,16},{16,18},{18... | collective-permute-start | bytes 195080 | tf_op jit(solution)/shard_map/ppermute | solution.py:12
  115.6 24.9 %collective-permute-start.12 = (f32[8,8192]{1,0:T(8,128)S(1)}, f32[8,8192]{1,0:T(8,128)S(1)}, u32[]{:S(2)}, u32[]{:S(2)}) collective-permute-start(f32[8,8192]{1,0:T(8,128)S(1)} %get-tuple-element.45), channel_id=1, source_target_pairs={{0,64},{64,128},{128,192},{192,0},{256,320},{320,384},{384,448},{4... | collective-permute-start | bytes 786440 | tf_op jit(solution)/shard_map/ppermute | solution.py:66
  120.6 19.9 %collective-permute-start.14 = (f32[8,8192]{1,0:T(8,128)S(1)}, f32[8,8192]{1,0:T(8,128)}, u32[]{:S(2)}, u32[]{:S(2)}) collective-permute-start(f32[8,8192]{1,0:T(8,128)S(1)} %get-tuple-element.46), channel_id=1, source_target_pairs={{0,192},{64,0},{128,64},{192,128},{256,448},{320,256},{384,320},{4... | collective-permute-start | bytes 786440 | tf_op jit(solution)/shard_map/ppermute | solution.py:66
  123.3 20.2 %collective-permute-start.13 = (f32[8,8192]{1,0:T(8,128)S(1)}, f32[8,8192]{1,0:T(8,128)}, u32[]{:S(2)}, u32[]{:S(2)}) collective-permute-start(f32[8,8192]{1,0:T(8,128)S(1)} %get-tuple-element.47), channel_id=1, source_target_pairs={{0,128},{64,192},{128,0},{192,64},{256,384},{320,448},{384,256},{4... | collective-permute-start | bytes 786440 | tf_op jit(solution)/shard_map/ppermute | solution.py:66
  126.4 5.8 %collective-permute-start.15 = (f32[16,128]{1,0:T(8,128)S(1)}, f32[16,128]{1,0:T(8,128)S(1)}, u32[]{:S(2)}, u32[]{:S(2)}) collective-permute-start(f32[16,128]{1,0:T(8,128)S(1)} %add.171), channel_id=1, source_target_pairs={{0,4},{2,6},{4,0},{6,2},{8,12},{10,14},{12,8},{14,10},{16,20},{18,... | collective-permute-start | bytes 24584 | tf_op jit(solution)/shard_map/ppermute | solution.py:29
  132.2 8.3 %collective-permute-start.16 = (f32[16,128]{1,0:T(8,128)S(1)}, f32[16,128]{1,0:T(8,128)S(1)}, u32[]{:S(2)}, u32[]{:S(2)}) collective-permute-start(f32[16,128]{1,0:T(8,128)S(1)} %add.181), channel_id=1, source_target_pairs={{0,8},{2,10},{4,12},{6,14},{8,0},{10,2},{12,4},{14,6},{16,24},{18,... | collective-permute-start | bytes 24584 | tf_op jit(solution)/shard_map/ppermute | solution.py:29
  145.2 12.5 %collective-permute-start.18 = (f32[16,128]{1,0:T(8,128)S(1)}, f32[16,128]{1,0:T(8,128)S(1)}, u32[]{:S(2)}, u32[]{:S(2)}) collective-permute-start(f32[16,128]{1,0:T(8,128)S(1)} %add.182), channel_id=1, source_target_pairs={{0,16},{2,18},{4,20},{6,22},{8,24},{10,26},{12,28},{14,30},{16,0},... | collective-permute-start | bytes 24584 | tf_op jit(solution)/shard_map/ppermute | solution.py:29
  157.7 18.0 %collective-permute-start.19 = (f32[16,128]{1,0:T(8,128)S(1)}, f32[16,128]{1,0:T(8,128)S(1)}, u32[]{:S(2)}, u32[]{:S(2)}) collective-permute-start(f32[16,128]{1,0:T(8,128)S(1)} %add.183), channel_id=1, source_target_pairs={{0,32},{2,34},{4,36},{6,38},{8,40},{10,42},{12,44},{14,46},{16,48}... | collective-permute-start | bytes 24584 | tf_op jit(solution)/shard_map/ppermute | solution.py:29
  (1 other events, 1.3 us)

commit v6 on v4

--- a/solution.py
+++ b/solution.py
@@ -174,7 +174,8 @@
     else:
         context_steps = [1 << k for k in range(lax.axis_size("context").bit_length() - 1)]
         dp_steps = [1 << k for k in range(lax.axis_size("dp").bit_length() - 1)]
-        first, second, third = context_steps[:1], context_steps[1:3], context_steps[3:]
+        context_steps = context_steps[::-1]
+        first, second, third = context_steps[:2], context_steps[2:4], context_steps[4:]
         summed = butterfly_rounds(butterfly_rounds(local_grad, "dp", dp_steps), "context", first)
         x_sums = scatter_stage(x_chunks, "tensor", inner, True, False)
         x_sums, summed = lax.optimization_barrier((x_sums, summed))

time: 169 us -> 175 us (1.036)
  waiting for transfers between devices: 24.9 us -> 37 us
  starting transfers between devices: 99.9 us -> 95.5 us
  local copies, waits for them, and re-layouts: 16.2 us -> 14.3 us
    ppermute x6, waiting for transfers between devices: 5.38 us -> 13 us  [scatter_stage(): lax.ppermute(sent, axis, grid_shift(axis, s, inner, outer_step))]
    ppermute x6, starting transfers between devices: 57.3 us -> 50.9 us  [butterfly_rounds(): lax.ppermute(value, axis, [(i, i ^ step) for i in range(count)])]
    ppermute x6, waiting for transfers between devices: 2.86 us -> 7.37 us  [butterfly_rounds(): lax.ppermute(value, axis, [(i, i ^ step) for i in range(count)])]
    ppermute x2, starting transfers between devices: 3.6 us -> 6.31 us  [from_behind(): lax.ppermute(value, axis, [(source, source + steps) for source in range(f...]
  transfers between devices with their start and end apart: 20 -> 20, of which waited for: 9 -> 9; matrix products, arithmetic and copies ran while one was open for 12% -> 10% of each run, Pallas kernels for 0% -> 0%
where the time goes in v6:
time: 175 us; the launch traced here: 172 us
  starting transfers between devices  95.5 us (55%)
  waiting for transfers between devices  37 us (21%)
  local copies, waits for them, and re-layouts  14.3 us (8%)
  matrix products  12.4 us (7%)
  other arithmetic  11.1 us (6%)
    ppermute x6, starting transfers between devices, butterfly_rounds(): lax.ppermute(value, axis, [(i, i ^ step) for i in range(count)])  50.9 us
    ppermute x6, starting transfers between devices, scatter_stage(): lax.ppermute(sent, axis, grid_shift(axis, s, inner, outer_step))  18.7 us
    ppermute x6, waiting for transfers between devices, scatter_stage(): lax.ppermute(sent, axis, grid_shift(axis, s, inner, outer_step))  13 us
    ppermute x3, waiting for transfers between devices, grid_gather(): lax.ppermute(stage, axis, grid_shift(axis, s, inner, True))  12.9 us
    ppermute x3, starting transfers between devices, grid_gather(): lax.ppermute(rows, axis, grid_shift(axis, s, inner, False))  10.3 us
    ppermute x3, starting transfers between devices, grid_gather(): lax.ppermute(stage, axis, grid_shift(axis, s, inner, True))  9.33 us
    ppermute x6, waiting for transfers between devices, butterfly_rounds(): lax.ppermute(value, axis, [(i, i ^ step) for i in range(count)])  7.37 us
    ppermute x2, starting transfers between devices, from_behind(): lax.ppermute(value, axis, [(source, source + steps) for source in range(f...  6.31 us
  transfers between devices with their start and end apart: 20, of which 9 were waited for; matrix products, arithmetic and copies ran while one was open for 10% of the time, Pallas kernels for 0%

profile of v6, /device:TPU:1, one launch (start us, length us, event | category | flops | bytes accessed | tf_op | source)
XLA Modules:
  0.0 171.8 jit_solution(349786230218689191)
XLA Ops:
  0.6 6.0 %collective-permute-start.3 = (bf16[8,8192]{1,0:T(8,128)(2,1)}, bf16[8,8192]{1,0:T(8,128)(2,1)S(1)}, u32[]{:S(2)}, u32[]{:S(2)}) collective-permute-start(bf16[8,8192]{1,0:T(8,128)(2,1)} %bitcast.118), channel_id=1, source_target_pairs={{0,192},{64,0},{128,64},{192,128},{256,448},{320,256},{384,320},{4... | collective-permute-start | bytes 393224 | tf_op jit(solution)/shard_map/ppermute | solution.py:45
  18.2 3.7 %collective-permute-done = bf16[1,127,256]{1,2,0:T(8,128)(2,1)S(1)} collective-permute-done((bf16[1,127,256]{1,2,0:T(8,128)(2,1)S(1)}, bf16[1,127,256]{1,2,0:T(8,128)(2,1)S(1)}, u32[]{:S(2)}, u32[]{:S(2)}) %collective-permute-start) | collective-permute-done | bytes 65056 | tf_op jit(solution)/shard_map/ppermute | solution.py:12
  23.3 4.4 %collective-permute-start.6 = (bf16[4,8,8192]{2,1,0:T(8,128)(2,1)S(1)}, bf16[4,8,8192]{2,1,0:T(8,128)(2,1)S(1)}, u32[]{:S(2)}, u32[]{:S(2)}) collective-permute-start(bf16[4,8,8192]{2,1,0:T(8,128)(2,1)S(1)} %broadcast_select_fusion), channel_id=1, source_target_pairs={{0,768},{64,832},{128,896},{192,960},{256,0},{320,64},{384,128},{4... | collective-permute-start | bytes 1572872 | tf_op jit(solution)/shard_map/ppermute | solution.py:50
  27.7 2.4 %collective-permute-start.5 = (bf16[4,8,8192]{2,1,0:T(8,128)(2,1)S(1)}, bf16[4,8,8192]{2,1,0:T(8,128)(2,1)S(1)}, u32[]{:S(2)}, u32[]{:S(2)}) collective-permute-start(bf16[4,8,8192]{2,1,0:T(8,128)(2,1)S(1)} %broadcast_select_fusion), channel_id=1, source_target_pairs={{0,512},{64,576},{128,640},{192,704},{256,768},{320,832},{384,896}... | collective-permute-start | bytes 1572872 | tf_op jit(solution)/shard_map/ppermute | solution.py:50
  30.2 2.5 %collective-permute-start.4 = (bf16[4,8,8192]{2,1,0:T(8,128)(2,1)S(1)}, bf16[4,8,8192]{2,1,0:T(8,128)(2,1)S(1)}, u32[]{:S(2)}, u32[]{:S(2)}) collective-permute-start(bf16[4,8,8192]{2,1,0:T(8,128)(2,1)S(1)} %broadcast_select_fusion), channel_id=1, source_target_pairs={{0,256},{64,320},{128,384},{192,448},{256,512},{320,576},{384,640}... | collective-permute-start | bytes 1572872 | tf_op jit(solution)/shard_map/ppermute | solution.py:50
  32.8 7.5 %collective-permute-done.6 = bf16[4,8,8192]{2,1,0:T(8,128)(2,1)S(1)} collective-permute-done((bf16[4,8,8192]{2,1,0:T(8,128)(2,1)S(1)}, bf16[4,8,8192]{2,1,0:T(8,128)(2,1)S(1)}, u32[]{:S(2)}, u32[]{:S(2)}) %collective-permute-start.6) | collective-permute-done | bytes 524320 | tf_op jit(solution)/shard_map/ppermute | solution.py:50
  40.3 5.3 %collective-permute-done.4 = bf16[4,8,8192]{2,1,0:T(8,128)(2,1)S(1)} collective-permute-done((bf16[4,8,8192]{2,1,0:T(8,128)(2,1)S(1)}, bf16[4,8,8192]{2,1,0:T(8,128)(2,1)S(1)}, u32[]{:S(2)}, u32[]{:S(2)}) %collective-permute-start.4) | collective-permute-done | bytes 524320 | tf_op jit(solution)/shard_map/ppermute | solution.py:50
  49.8 4.7 %fusion.5 = bf16[128,2,256]{2,0,1:T(8,128)(2,1)S(1)} fusion(bf16[8192,2,256]{2,1,0:T(2,128)(2,1)} %param.10, bf16[128,8192]{1,0:T(8,128)(2,1)S(1)} %bitcast_select_fusion), kind=kOutput, calls=%fused_computation.11 | convolution fusion | flops 1073807360 | bytes 10616832 | tf_op jit(solution)/shard_map/nd,djc->njc/dot_general | solution.py:114
  55.1 6.3 %fusion = bf16[128,8192]{1,0:T(8,128)(2,1)S(1)} fusion(bf16[8192,2,256]{2,1,0:T(2,128)(2,1)} %param.10, bf16[128,1,256]{2,0,1:T(8,128)(2,1)S(1)} %get-tuple-element.45, bf16[128,1,256]{2,0,1:T(8,128)(2,1)S(1)} %get-tuple-element.44), kind=kOutput, calls=%fused_computation.3 | convolution fusion | flops 1074855936 | bytes 10616832 | tf_op jit(solution)/shard_map/bnjc,djc->bnd/dot_general | solution.py:151
  62.6 3.9 %collective-permute-start.7 = (bf16[32,8192]{1,0:T(8,128)(2,1)}, bf16[32,8192]{1,0:T(8,128)(2,1)}, u32[]{:S(2)}, u32[]{:S(2)}) collective-permute-start(bf16[32,8192]{1,0:T(8,128)(2,1)} %get-tuple-element.38), channel_id=1, source_target_pairs={{0,256},{64,320},{128,384},{192,448},{256,512},{320,576},{384,640}... | collective-permute-start | bytes 1572872 | tf_op jit(solution)/shard_map/ppermute | solution.py:66
  66.5 2.6 %collective-permute-start.9 = (bf16[32,8192]{1,0:T(8,128)(2,1)}, bf16[32,8192]{1,0:T(8,128)(2,1)}, u32[]{:S(2)}, u32[]{:S(2)}) collective-permute-start(bf16[32,8192]{1,0:T(8,128)(2,1)} %get-tuple-element.39), channel_id=1, source_target_pairs={{0,768},{64,832},{128,896},{192,960},{256,0},{320,64},{384,128},{4... | collective-permute-start | bytes 1572872 | tf_op jit(solution)/shard_map/ppermute | solution.py:66
  69.1 3.0 %collective-permute-start.8 = (bf16[32,8192]{1,0:T(8,128)(2,1)}, bf16[32,8192]{1,0:T(8,128)(2,1)}, u32[]{:S(2)}, u32[]{:S(2)}) collective-permute-start(bf16[32,8192]{1,0:T(8,128)(2,1)} %get-tuple-element.40), channel_id=1, source_target_pairs={{0,512},{64,576},{128,640},{192,704},{256,768},{320,832},{384,896}... | collective-permute-start | bytes 1572872 | tf_op jit(solution)/shard_map/ppermute | solution.py:66
  74.0 3.6 %reshape.293 = f32[16,128,257]{2,1,0:T(8,128)} reshape(f32[16,32896]{1,0:T(8,128)S(1)} %pad.4) | data formatting | bytes 4210688 | tf_op jit(solution)/shard_map/reshape | solution.py:100
  79.8 12.4 %collective-permute-start.10 = (f32[16,128]{1,0:T(8,128)S(1)}, f32[16,128]{1,0:T(8,128)S(1)}, u32[]{:S(2)}, u32[]{:S(2)}) collective-permute-start(f32[16,128]{1,0:T(8,128)S(1)} %slice.68), channel_id=1, source_target_pairs={{0,1},{1,0},{2,3},{3,2},{4,5},{5,4},{6,7},{7,6},{8,9},{9,8},{10,11... | collective-permute-start | bytes 24584 | tf_op jit(solution)/shard_map/ppermute | solution.py:29
  93.0 19.0 %collective-permute-start.11 = (f32[16,128]{1,0:T(8,128)S(1)}, f32[16,128]{1,0:T(8,128)S(1)}, u32[]{:S(2)}, u32[]{:S(2)}) collective-permute-start(f32[16,128]{1,0:T(8,128)S(1)} %slice_add_fusion), channel_id=1, source_target_pairs={{0,32},{2,34},{4,36},{6,38},{8,40},{10,42},{12,44},{14,46},{16,48}... | collective-permute-start | bytes 24584 | tf_op jit(solution)/shard_map/ppermute | solution.py:29
  113.1 7.7 %collective-permute-start.12 = (f32[16,128]{1,0:T(8,128)S(1)}, f32[16,128]{1,0:T(8,128)S(1)}, u32[]{:S(2)}, u32[]{:S(2)}) collective-permute-start(f32[16,128]{1,0:T(8,128)S(1)} %add.171), channel_id=1, source_target_pairs={{0,16},{2,18},{4,20},{6,22},{8,24},{10,26},{12,28},{14,30},{16,0},... | collective-permute-start | bytes 24584 | tf_op jit(solution)/shard_map/ppermute | solution.py:29
  121.0 5.0 %collective-permute-start.18 = (bf16[1,127,256]{2,1,0:T(8,128)(2,1)S(1)}, bf16[1,127,256]{2,1,0:T(8,128)(2,1)S(1)}, u32[]{:S(2)}, u32[]{:S(2)}) collective-permute-start(bf16[1,127,256]{2,1,0:T(8,128)(2,1)S(1)} %slice.69), channel_id=1, source_target_pairs={{0,2},{2,4},{4,6},{6,8},{8,10},{10,12},{12,14},{14,16},{16,18},{18... | collective-permute-start | bytes 195080 | tf_op jit(solution)/shard_map/ppermute | solution.py:12
  127.9 4.1 %collective-permute-start.16 = (f32[16,128]{1,0:T(8,128)S(1)}, f32[16,128]{1,0:T(8,128)S(1)}, u32[]{:S(2)}, u32[]{:S(2)}) collective-permute-start(f32[16,128]{1,0:T(8,128)S(1)} %add.172), channel_id=1, source_target_pairs={{0,8},{2,10},{4,12},{6,14},{8,0},{10,2},{12,4},{14,6},{16,24},{18,... | collective-permute-start | bytes 24584 | tf_op jit(solution)/shard_map/ppermute | solution.py:29
  132.7 2.7 %collective-permute-start.13 = (f32[8,8192]{1,0:T(8,128)}, f32[8,8192]{1,0:T(8,128)S(1)}, u32[]{:S(2)}, u32[]{:S(2)}) collective-permute-start(f32[8,8192]{1,0:T(8,128)} %get-tuple-element.41), channel_id=1, source_target_pairs={{0,64},{64,128},{128,192},{192,0},{256,320},{320,384},{384,448},{4... | collective-permute-start | bytes 786440 | tf_op jit(solution)/shard_map/ppermute | solution.py:66
  135.5 4.3 %collective-permute-start.15 = (f32[8,8192]{1,0:T(8,128)S(1)}, f32[8,8192]{1,0:T(8,128)S(1)}, u32[]{:S(2)}, u32[]{:S(2)}) collective-permute-start(f32[8,8192]{1,0:T(8,128)S(1)} %get-tuple-element.42), channel_id=1, source_target_pairs={{0,192},{64,0},{128,64},{192,128},{256,448},{320,256},{384,320},{4... | collective-permute-start | bytes 786440 | tf_op jit(solution)/shard_map/ppermute | solution.py:66
  142.2 4.7 %collective-permute-start.17 = (f32[16,128]{1,0:T(8,128)S(1)}, f32[16,128]{1,0:T(8,128)S(1)}, u32[]{:S(2)}, u32[]{:S(2)}) collective-permute-start(f32[16,128]{1,0:T(8,128)S(1)} %add.182), channel_id=1, source_target_pairs={{0,4},{2,6},{4,0},{6,2},{8,12},{10,14},{12,8},{14,10},{16,20},{18,... | collective-permute-start | bytes 24584 | tf_op jit(solution)/shard_map/ppermute | solution.py:29
  150.3 10.9 %collective-permute-done.14 = f32[8,8192]{1,0:T(8,128)} collective-permute-done((f32[8,8192]{1,0:T(8,128)S(1)}, f32[8,8192]{1,0:T(8,128)}, u32[]{:S(2)}, u32[]{:S(2)}) %collective-permute-start.14) | collective-permute-done | bytes 262176 | tf_op jit(solution)/shard_map/ppermute | solution.py:66
  162.9 2.9 %collective-permute-start.19 = (f32[16,128]{1,0:T(8,128)S(1)}, f32[16,128]{1,0:T(8,128)S(1)}, u32[]{:S(2)}, u32[]{:S(2)}) collective-permute-start(f32[16,128]{1,0:T(8,128)S(1)} %add.183), channel_id=1, source_target_pairs={{0,2},{2,0},{4,6},{6,4},{8,10},{10,8},{12,14},{14,12},{16,18},{18,... | collective-permute-start | bytes 24584 | tf_op jit(solution)/shard_map/ppermute | solution.py:29
  166.6 4.6 %collective-permute-done.19 = f32[16,128]{1,0:T(8,128)S(1)} collective-permute-done((f32[16,128]{1,0:T(8,128)S(1)}, f32[16,128]{1,0:T(8,128)S(1)}, u32[]{:S(2)}, u32[]{:S(2)}) %collective-permute-start.19) | collective-permute-done | bytes 8224 | tf_op jit(solution)/shard_map/ppermute | solution.py:29
  (83 shorter events, 35.9 us)
Async XLA Ops:
  0.6 21.9 %collective-permute-start.3 = (bf16[8,8192]{1,0:T(8,128)(2,1)}, bf16[8,8192]{1,0:T(8,128)(2,1)S(1)}, u32[]{:S(2)}, u32[]{:S(2)}) collective-permute-start(bf16[8,8192]{1,0:T(8,128)(2,1)} %bitcast.118), channel_id=1, source_target_pairs={{0,192},{64,0},{128,64},{192,128},{256,448},{320,256},{384,320},{4... | collective-permute-start | bytes 393224 | tf_op jit(solution)/shard_map/ppermute | solution.py:45
  6.7 15.8 %collective-permute-start.2 = (bf16[8,8192]{1,0:T(8,128)(2,1)}, bf16[8,8192]{1,0:T(8,128)(2,1)S(1)}, u32[]{:S(2)}, u32[]{:S(2)}) collective-permute-start(bf16[8,8192]{1,0:T(8,128)(2,1)} %bitcast.119), channel_id=1, source_target_pairs={{0,128},{64,192},{128,0},{192,64},{256,384},{320,448},{384,256},{4... | collective-permute-start | bytes 393224 | tf_op jit(solution)/shard_map/ppermute | solution.py:45
  8.6 13.9 %collective-permute-start.1 = (bf16[8,8192]{1,0:T(8,128)(2,1)}, bf16[8,8192]{1,0:T(8,128)(2,1)S(1)}, u32[]{:S(2)}, u32[]{:S(2)}) collective-permute-start(bf16[8,8192]{1,0:T(8,128)(2,1)} %bitcast.120), channel_id=1, source_target_pairs={{0,64},{64,128},{128,192},{192,0},{256,320},{320,384},{384,448},{4... | collective-permute-start | bytes 393224 | tf_op jit(solution)/shard_map/ppermute | solution.py:45
  12.9 9.0 %collective-permute-start = (bf16[1,127,256]{1,2,0:T(8,128)(2,1)S(1)}, bf16[1,127,256]{1,2,0:T(8,128)(2,1)S(1)}, u32[]{:S(2)}, u32[]{:S(2)}) collective-permute-start(bf16[1,127,256]{1,2,0:T(8,128)(2,1)S(1)} %bitcast.105), channel_id=1, source_target_pairs={{2,0},{4,2},{6,4},{8,6},{10,8},{12,10},{14,12},{16,14},{18,16},{20... | collective-permute-start | bytes 195080 | tf_op jit(solution)/shard_map/ppermute | solution.py:12
  17.9 4.6 %copy-start.1 = (bf16[1,1,8,8192]{3,2,1,0:T(8,128)(2,1)S(1)}, bf16[1,1,8,8192]{3,2,1,0:T(8,128)(2,1)}, u32[]{:S(2)}) copy-start(bf16[1,1,8,8192]{3,2,1,0:T(8,128)(2,1)} %param.9) | copy-start | bytes 393220
  23.3 17.0 %collective-permute-start.6 = (bf16[4,8,8192]{2,1,0:T(8,128)(2,1)S(1)}, bf16[4,8,8192]{2,1,0:T(8,128)(2,1)S(1)}, u32[]{:S(2)}, u32[]{:S(2)}) collective-permute-start(bf16[4,8,8192]{2,1,0:T(8,128)(2,1)S(1)} %broadcast_select_fusion), channel_id=1, source_target_pairs={{0,768},{64,832},{128,896},{192,960},{256,0},{320,64},{384,128},{4... | collective-permute-start | bytes 1572872 | tf_op jit(solution)/shard_map/ppermute | solution.py:50
  27.7 12.6 %collective-permute-start.5 = (bf16[4,8,8192]{2,1,0:T(8,128)(2,1)S(1)}, bf16[4,8,8192]{2,1,0:T(8,128)(2,1)S(1)}, u32[]{:S(2)}, u32[]{:S(2)}) collective-permute-start(bf16[4,8,8192]{2,1,0:T(8,128)(2,1)S(1)} %broadcast_select_fusion), channel_id=1, source_target_pairs={{0,512},{64,576},{128,640},{192,704},{256,768},{320,832},{384,896}... | collective-permute-start | bytes 1572872 | tf_op jit(solution)/shard_map/ppermute | solution.py:50
  30.2 15.5 %collective-permute-start.4 = (bf16[4,8,8192]{2,1,0:T(8,128)(2,1)S(1)}, bf16[4,8,8192]{2,1,0:T(8,128)(2,1)S(1)}, u32[]{:S(2)}, u32[]{:S(2)}) collective-permute-start(bf16[4,8,8192]{2,1,0:T(8,128)(2,1)S(1)} %broadcast_select_fusion), channel_id=1, source_target_pairs={{0,256},{64,320},{128,384},{192,448},{256,512},{320,576},{384,640}... | collective-permute-start | bytes 1572872 | tf_op jit(solution)/shard_map/ppermute | solution.py:50
  61.3 11.3 %copy-start = (bf16[128,8192]{1,0:T(8,128)(2,1)}, bf16[128,8192]{1,0:T(8,128)(2,1)S(1)}, u32[]{:S(2)}) copy-start(bf16[128,8192]{1,0:T(8,128)(2,1)S(1)} %fusion) | copy-start | bytes 6291460
  62.6 63.4 %collective-permute-start.7 = (bf16[32,8192]{1,0:T(8,128)(2,1)}, bf16[32,8192]{1,0:T(8,128)(2,1)}, u32[]{:S(2)}, u32[]{:S(2)}) collective-permute-start(bf16[32,8192]{1,0:T(8,128)(2,1)} %get-tuple-element.38), channel_id=1, source_target_pairs={{0,256},{64,320},{128,384},{192,448},{256,512},{320,576},{384,640}... | collective-permute-start | bytes 1572872 | tf_op jit(solution)/shard_map/ppermute | solution.py:66
  66.5 59.5 %collective-permute-start.9 = (bf16[32,8192]{1,0:T(8,128)(2,1)}, bf16[32,8192]{1,0:T(8,128)(2,1)}, u32[]{:S(2)}, u32[]{:S(2)}) collective-permute-start(bf16[32,8192]{1,0:T(8,128)(2,1)} %get-tuple-element.39), channel_id=1, source_target_pairs={{0,768},{64,832},{128,896},{192,960},{256,0},{320,64},{384,128},{4... | collective-permute-start | bytes 1572872 | tf_op jit(solution)/shard_map/ppermute | solution.py:66
  69.1 56.9 %collective-permute-start.8 = (bf16[32,8192]{1,0:T(8,128)(2,1)}, bf16[32,8192]{1,0:T(8,128)(2,1)}, u32[]{:S(2)}, u32[]{:S(2)}) collective-permute-start(bf16[32,8192]{1,0:T(8,128)(2,1)} %get-tuple-element.40), channel_id=1, source_target_pairs={{0,512},{64,576},{128,640},{192,704},{256,768},{320,832},{384,896}... | collective-permute-start | bytes 1572872 | tf_op jit(solution)/shard_map/ppermute | solution.py:66
  79.8 13.2 %collective-permute-start.10 = (f32[16,128]{1,0:T(8,128)S(1)}, f32[16,128]{1,0:T(8,128)S(1)}, u32[]{:S(2)}, u32[]{:S(2)}) collective-permute-start(f32[16,128]{1,0:T(8,128)S(1)} %slice.68), channel_id=1, source_target_pairs={{0,1},{1,0},{2,3},{3,2},{4,5},{5,4},{6,7},{7,6},{8,9},{9,8},{10,11... | collective-permute-start | bytes 24584 | tf_op jit(solution)/shard_map/ppermute | solution.py:29
  93.0 20.1 %collective-permute-start.11 = (f32[16,128]{1,0:T(8,128)S(1)}, f32[16,128]{1,0:T(8,128)S(1)}, u32[]{:S(2)}, u32[]{:S(2)}) collective-permute-start(f32[16,128]{1,0:T(8,128)S(1)} %slice_add_fusion), channel_id=1, source_target_pairs={{0,32},{2,34},{4,36},{6,38},{8,40},{10,42},{12,44},{14,46},{16,48}... | collective-permute-start | bytes 24584 | tf_op jit(solution)/shard_map/ppermute | solution.py:29
  113.1 12.9 %collective-permute-start.12 = (f32[16,128]{1,0:T(8,128)S(1)}, f32[16,128]{1,0:T(8,128)S(1)}, u32[]{:S(2)}, u32[]{:S(2)}) collective-permute-start(f32[16,128]{1,0:T(8,128)S(1)} %add.171), channel_id=1, source_target_pairs={{0,16},{2,18},{4,20},{6,22},{8,24},{10,26},{12,28},{14,30},{16,0},... | collective-permute-start | bytes 24584 | tf_op jit(solution)/shard_map/ppermute | solution.py:29
  121.0 20.9 %collective-permute-start.18 = (bf16[1,127,256]{2,1,0:T(8,128)(2,1)S(1)}, bf16[1,127,256]{2,1,0:T(8,128)(2,1)S(1)}, u32[]{:S(2)}, u32[]{:S(2)}) collective-permute-start(bf16[1,127,256]{2,1,0:T(8,128)(2,1)S(1)} %slice.69), channel_id=1, source_target_pairs={{0,2},{2,4},{4,6},{6,8},{8,10},{10,12},{12,14},{14,16},{16,18},{18... | collective-permute-start | bytes 195080 | tf_op jit(solution)/shard_map/ppermute | solution.py:12
  127.9 14.3 %collective-permute-start.16 = (f32[16,128]{1,0:T(8,128)S(1)}, f32[16,128]{1,0:T(8,128)S(1)}, u32[]{:S(2)}, u32[]{:S(2)}) collective-permute-start(f32[16,128]{1,0:T(8,128)S(1)} %add.172), channel_id=1, source_target_pairs={{0,8},{2,10},{4,12},{6,14},{8,0},{10,2},{12,4},{14,6},{16,24},{18,... | collective-permute-start | bytes 24584 | tf_op jit(solution)/shard_map/ppermute | solution.py:29
  132.7 15.4 %collective-permute-start.13 = (f32[8,8192]{1,0:T(8,128)}, f32[8,8192]{1,0:T(8,128)S(1)}, u32[]{:S(2)}, u32[]{:S(2)}) collective-permute-start(f32[8,8192]{1,0:T(8,128)} %get-tuple-element.41), channel_id=1, source_target_pairs={{0,64},{64,128},{128,192},{192,0},{256,320},{320,384},{384,448},{4... | collective-permute-start | bytes 786440 | tf_op jit(solution)/shard_map/ppermute | solution.py:66
  135.5 14.9 %collective-permute-start.15 = (f32[8,8192]{1,0:T(8,128)S(1)}, f32[8,8192]{1,0:T(8,128)S(1)}, u32[]{:S(2)}, u32[]{:S(2)}) collective-permute-start(f32[8,8192]{1,0:T(8,128)S(1)} %get-tuple-element.42), channel_id=1, source_target_pairs={{0,192},{64,0},{128,64},{192,128},{256,448},{320,256},{384,320},{4... | collective-permute-start | bytes 786440 | tf_op jit(solution)/shard_map/ppermute | solution.py:66
  139.8 21.4 %collective-permute-start.14 = (f32[8,8192]{1,0:T(8,128)S(1)}, f32[8,8192]{1,0:T(8,128)}, u32[]{:S(2)}, u32[]{:S(2)}) collective-permute-start(f32[8,8192]{1,0:T(8,128)S(1)} %get-tuple-element.43), channel_id=1, source_target_pairs={{0,128},{64,192},{128,0},{192,64},{256,384},{320,448},{384,256},{4... | collective-permute-start | bytes 786440 | tf_op jit(solution)/shard_map/ppermute | solution.py:66
  142.2 6.0 %collective-permute-start.17 = (f32[16,128]{1,0:T(8,128)S(1)}, f32[16,128]{1,0:T(8,128)S(1)}, u32[]{:S(2)}, u32[]{:S(2)}) collective-permute-start(f32[16,128]{1,0:T(8,128)S(1)} %add.182), channel_id=1, source_target_pairs={{0,4},{2,6},{4,0},{6,2},{8,12},{10,14},{12,8},{14,10},{16,20},{18,... | collective-permute-start | bytes 24584 | tf_op jit(solution)/shard_map/ppermute | solution.py:29
  162.9 8.3 %collective-permute-start.19 = (f32[16,128]{1,0:T(8,128)S(1)}, f32[16,128]{1,0:T(8,128)S(1)}, u32[]{:S(2)}, u32[]{:S(2)}) collective-permute-start(f32[16,128]{1,0:T(8,128)S(1)} %add.183), channel_id=1, source_target_pairs={{0,2},{2,0},{4,6},{6,4},{8,10},{10,8},{12,14},{14,12},{16,18},{18,... | collective-permute-start | bytes 24584 | tf_op jit(solution)/shard_map/ppermute | solution.py:29
